TPU v7x, 512 devices: a whole 4x8x8 slice. The times are simulated.
512 devices in a mesh: node: 32 (over x, y), tile: 16 (over z, core).
Axes of the slice: x: 4, y: 8, z: 8, core: 2. Of those that a mesh axis runs over, the one named last changes fastest.
Arguments:
- states: bfloat16 [196608, 128], P(('node', 'tile')), may hold values from -6 to 6
- adjacency: bfloat16 [65536, 128, 128], P(('node', 'tile')), may hold values from -0.5 to 0.5
- tile_node: int32 [512, 128], P(('node', 'tile')), may hold values from 0 to 31
- tile_block: int32 [512, 128], P(('node', 'tile')), may hold values from 0 to 1, as said below
- tile_rel: int32 [512, 128], P(('node', 'tile')), may hold values from 0 to 534
- tile_dst: int32 [512, 128], P(('node', 'tile')), may hold values from 0 to 47
- send_blocks: int32 [512, 32, 2], P(('node', 'tile')), may hold values from 0 to 2
- send_count: int32 [512, 32], P(('node', 'tile')), may hold values from 1 to 2, as said below
- active: int32 [2, 1536], P(None, ('node', 'tile')), may hold values 0 or 1
- relations: bfloat16 [535, 128], replicated, may hold values from -6 to 6
- mix_weight: bfloat16 [2, 64, 64], replicated, may hold values from -0.75 to 0.75
- norm_gain: float32 [2, 64], replicated, may hold values from 0.5 to 1.5
Outputs:
- new_states: bfloat16 [196608, 128], P(('node', 'tile'))
Inputs may be any that keep to these rules, and one draw needn't show every extreme that they name: On each device, the first send_count entries of each list are distinct; every device has one list with all 2 slots used. For tile t of device n * 16 + j, tile_block[d, t] is less than send_count[a * 16 + j, n], where a = tile_node[d, t].
All inputs are finite; a program needn't handle non-finite values. No bound on the sum of `active` on one device may be relied on, other than what follows from the above.
Results may differ from a plain program's by a relative error of at most 0.02.
Values may be sent and summed in bfloat16 or wider, within the bound.
No kernel may reach another device: no remote copies, remote signals or barrier semaphores. Data moves between devices by JAX's collectives and lax.ppermute only.
A program may use at most 64 MiB of HBM per device.

v0:
```python
import jax
import jax.numpy as jnp
from jax import lax
from jax.sharding import PartitionSpec as P


def body(
    states,
    adjacency,
    tile_node,
    tile_block,
    tile_rel,
    tile_dst,
    send_blocks,
    send_count,
    active,
    relations,
    mix_weight,
    norm_gain,
):
    size_block = adjacency.shape[1]
    width = states.shape[1]
    own_blocks = states.shape[0] // size_block
    group_blocks = own_blocks * lax.axis_size("tile")
    tiles_here = adjacency.shape[0]
    capacity = send_blocks.shape[2]
    depth = mix_weight.shape[1]
    query_count = width // depth
    rel_onehot = (
        tile_rel[0][:, None] == jnp.arange(relations.shape[0], dtype=jnp.int32)[None, :]
    ).astype(jnp.bfloat16)
    rel_rows = jnp.dot(rel_onehot, relations, preferred_element_type=jnp.float32)
    dst_onehot = (
        jnp.arange(group_blocks, dtype=jnp.int32)[:, None] == tile_dst[0][None, :]
    ).astype(jnp.bfloat16)
    for layer in range(mix_weight.shape[0]):
        blocks = states.reshape(own_blocks, size_block, width) * active[layer][
            :, None, None
        ].astype(jnp.bfloat16)
        usable = jnp.arange(capacity, dtype=jnp.int32)[None, :] < send_count[0][:, None]
        picked = jnp.take(blocks, send_blocks[0], axis=0)
        picked = jnp.where(usable[:, :, None, None], picked, jnp.zeros_like(picked))
        arrived = lax.all_to_all(picked, "node", split_axis=0, concat_axis=0, tiled=True)
        slot_index = tile_node[0] * capacity + tile_block[0]
        source = arrived.reshape(-1, size_block, width)
        source_rows = jnp.take(source, slot_index, axis=0)
        modulated = (source_rows * rel_rows[:, None, :]).astype(jnp.bfloat16)
        products = jnp.einsum(
            "tij,tjf->tif", adjacency, modulated, preferred_element_type=jnp.float32
        )
        flat_products = products.reshape(tiles_here, -1)
        high_part = flat_products.astype(jnp.bfloat16)
        low_part = (flat_products - high_part.astype(jnp.float32)).astype(jnp.bfloat16)
        partial_sum = jnp.dot(dst_onehot, high_part, preferred_element_type=jnp.float32) + jnp.dot(
            dst_onehot, low_part, preferred_element_type=jnp.float32
        )
        partial_sum = lax.optimization_barrier(partial_sum.astype(jnp.bfloat16)).astype(jnp.float32)
        summed = lax.psum_scatter(
            partial_sum.reshape(group_blocks * size_block, width).astype(jnp.bfloat16),
            "tile",
            scatter_dimension=0,
            tiled=True,
        )
        mixer = jnp.kron(jnp.eye(query_count, dtype=jnp.bfloat16), mix_weight[layer])
        mixed = jnp.dot(summed, mixer, preferred_element_type=jnp.float32).reshape(
            -1, query_count, depth
        )
        center = jnp.mean(mixed, axis=-1, keepdims=True)
        spread = jnp.mean(jnp.square(mixed - center), axis=-1, keepdims=True)
        normed = (mixed - center) * lax.rsqrt(spread + 1e-05) * norm_gain[layer]
        states = (states.astype(jnp.float32) + jax.nn.relu(normed).reshape(-1, width)).astype(
            jnp.bfloat16
        )
    return states


def solution(mesh):
    placed = (
        P(("node", "tile"), None),
        P(("node", "tile"), None, None),
        P(("node", "tile"), None),
        P(("node", "tile"), None),
        P(("node", "tile"), None),
        P(("node", "tile"), None),
        P(("node", "tile"), None, None),
        P(("node", "tile"), None),
        P(None, ("node", "tile")),
        P(),
        P(),
        P(),
    )
    return jax.shard_map(
        body, mesh=mesh, in_specs=placed, out_specs=P(("node", "tile"), None), check_vma=False
    )
```

profile of v0, /device:TPU:1, one launch (start us, length us, event | category | flops | bytes accessed | tf_op | source)
XLA Modules:
  0.0 324.7 jit_solution(4121088416059537222)
XLA Ops:
  9.7 1.0 broadcast_multiply_fusion.1
  11.6 1.7 select_select_fusion.1
  13.3 10.5 %all-to-all-start = ((bf16[32,2,128,128]{3,2,1,0:T(8,128)(2,1)}), bf16[32,2,128,128]{3,2,1,0:T(8,128)(2,1)S(1)}, u32[]{:S(2)}, u32[]{:S(2)}) async-start(bf16[32,2,128,128]{3,2,1,0:T(8,128)(2,1)} %select_select_fusion.1), calls=%async_computation | async-start | bytes 4194304 | tf_op jit(solution)/shard_map/all_to_all | solution.py:43
  24.2 48.5 %all-to-all-done = bf16[32,2,128,128]{3,2,1,0:T(8,128)(2,1)S(1)} async-done(((bf16[32,2,128,128]{3,2,1,0:T(8,128)(2,1)}), bf16[32,2,128,128]{3,2,1,0:T(8,128)(2,1)S(1)}, u32[]{:S(2)}, u32[]{:S(2)}) %all-to-all-start) | async-done | bytes 2097184 | tf_op jit(solution)/shard_map/all_to_all | solution.py:43
  72.7 3.0 gather_fusion.1
  75.7 9.2 %fusion.13 = f32[128,128,128]{1,2,0:T(8,128)} fusion(bf16[128,128,128]{2,1,0:T(8,128)(2,1)} %param.17, bf16[128,128,128]{2,1,0:T(8,128)(2,1)} %gather_fusion.1, f32[128,128]{1,0:T(8,128)S(1)} %fusion.16, pred[128]{0:T(512)(128)(4,1)S(1)} %get-tuple-element.11), kind=kOutput, calls=%fused_computation.25 | convolution fusion | flops 545259520 | bytes 16842880 | tf_op jit(solution)/shard_map/tij,tjf->tif/dot_general | solution.py:48
  85.0 9.4 %copy.24 = f32[128,128,128]{0,2,1:T(8,128)} copy(f32[128,128,128]{1,2,0:T(8,128)} %fusion.13) | data formatting | bytes 16777216 | tf_op jit(solution)/shard_map/tij,tjf->tif/dot_general | solution.py:48
  94.4 4.0 %fusion.3 = (bf16[128,16384]{0,1:T(8,128)(2,1)S(1)}, bf16[128,16384]{0,1:T(8,128)(2,1)S(1)}) fusion(f32[128,128,128]{0,2,1:T(8,128)} %copy.24), kind=kLoop, calls=%fused_computation.13 | loop fusion | flops 8388608 | bytes 16777216 | tf_op jit(solution)/shard_map/convert_element_type | solution.py:53
  98.4 1.5 fusion.23
  100.0 1.5 fusion
  101.6 2.1 convert_element_type.96
  104.3 61.6 %reduce-scatter.3.cloned.1.call-done = bf16[384,128]{1,0:T(8,128)(2,1)} async-done(((bf16[6144,128]{1,0:T(8,128)(2,1)}), bf16[384,128]{1,0:T(8,128)(2,1)}) %reduce-scatter.3.cloned.1.call-update) | async-done | bytes 98320 | tf_op jit(solution)/shard_map/reduce_scatter | solution.py:58
  165.9 1.1 fusion.30
  167.4 0.9 gather_fusion.2
  168.7 52.9 %all_to_all.10 = bf16[32,2,128,128]{3,2,1,0:T(8,128)(2,1)S(1)} all-to-all(bf16[32,2,128,128]{3,2,1,0:T(8,128)(2,1)S(1)} %select_select_fusion), channel_id=1, replica_groups=mesh['node'=32,'tile'=16] {'node'}, dimensions={0} | all-to-all | bytes 4194304 | tf_op jit(solution)/shard_map/all_to_all | solution.py:43
  221.6 3.0 gather_fusion.3
  224.6 9.2 %fusion.12 = f32[128,128,128]{1,2,0:T(8,128)} fusion(bf16[128,128,128]{2,1,0:T(8,128)(2,1)} %param.17, bf16[128,128,128]{2,1,0:T(8,128)(2,1)} %gather_fusion.3, f32[128,128]{1,0:T(8,128)S(1)} %fusion.16, pred[128]{0:T(512)(128)(4,1)S(1)} %get-tuple-element.11), kind=kOutput, calls=%fused_computation.24 | convolution fusion | flops 545259520 | bytes 16842880 | tf_op jit(solution)/shard_map/tij,tjf->tif/dot_general | solution.py:48
  233.9 9.4 %copy.30 = f32[128,128,128]{0,2,1:T(8,128)} copy(f32[128,128,128]{1,2,0:T(8,128)} %fusion.12) | data formatting | bytes 16777216 | tf_op jit(solution)/shard_map/tij,tjf->tif/dot_general | solution.py:48
  243.3 4.0 %fusion.2 = (bf16[128,16384]{0,1:T(8,128)(2,1)S(1)}, bf16[128,16384]{0,1:T(8,128)(2,1)S(1)}) fusion(f32[128,128,128]{0,2,1:T(8,128)} %copy.30), kind=kLoop, calls=%fused_computation.10 | loop fusion | flops 8388608 | bytes 16777216 | tf_op jit(solution)/shard_map/convert_element_type | solution.py:53
  247.3 1.5 fusion.22
  248.9 1.5 fusion.1
  250.4 2.1 convert_element_type.107
  252.7 63.1 %reduce-scatter.5.cloned.1.call-done = bf16[384,128]{1,0:T(8,128)(2,1)} async-done(((bf16[6144,128]{1,0:T(8,128)(2,1)}), bf16[384,128]{1,0:T(8,128)(2,1)}) %reduce-scatter.5.cloned.1.call-update) | async-done | bytes 98320 | tf_op jit(solution)/shard_map/reduce_scatter | solution.py:58
  315.8 1.1 fusion.31
  (57 shorter events, 6.7 us)
Async XLA Ops:
  6.5 17.4 %copy-start = (bf16[535,128]{1,0:T(8,128)(2,1)S(1)}, bf16[535,128]{1,0:T(8,128)(2,1)}, u32[]{:S(2)}) copy-start(bf16[535,128]{1,0:T(8,128)(2,1)} %param.25) | copy-start | bytes 410884
  11.6 12.3 %copy-start.6 = (s32[1,128]{1,0:T(1,128)S(1)}, s32[1,128]{1,0:T(1,128)}, u32[]{:S(2)}) copy-start(s32[1,128]{1,0:T(1,128)} %param.19) | copy-start | bytes 1540
  11.6 12.3 %copy-start.7 = (s32[1,128]{1,0:T(1,128)S(1)}, s32[1,128]{1,0:T(1,128)}, u32[]{:S(2)}) copy-start(s32[1,128]{1,0:T(1,128)} %param.18) | copy-start | bytes 1540
  11.6 12.3 %copy-start.8 = (s32[1,128]{1,0:T(1,128)S(1)}, s32[1,128]{1,0:T(1,128)}, u32[]{:S(2)}) copy-start(s32[1,128]{1,0:T(1,128)} %param.20) | copy-start | bytes 1540
  13.3 59.4 %all-to-all-start = ((bf16[32,2,128,128]{3,2,1,0:T(8,128)(2,1)}), bf16[32,2,128,128]{3,2,1,0:T(8,128)(2,1)S(1)}, u32[]{:S(2)}, u32[]{:S(2)}) async-start(bf16[32,2,128,128]{3,2,1,0:T(8,128)(2,1)} %select_select_fusion.1), calls=%async_computation | async-start | bytes 4194304 | tf_op jit(solution)/shard_map/all_to_all | solution.py:43
  23.8 142.0 %reduce-scatter.3.cloned.1.call-start = ((), (), s32[]{:S(2)}) async-start(), calls=%async_computation.4 | async-start | bytes 1671168 | tf_op jit(solution)/shard_map/reduce_scatter | solution.py:58
  94.4 4.0 %copy-start.4 = (s32[1,128]{1,0:T(1,128)S(1)}, s32[1,128]{1,0:T(1,128)}, u32[]{:S(2)}) copy-start(s32[1,128]{1,0:T(1,128)} %param.21) | copy-start | bytes 1540
  101.5 2.2 copy-start.3
  101.6 2.7 copy-start.5
  101.6 65.7 %copy-start.2 = (bf16[384,128]{1,0:T(8,128)(2,1)S(1)}, bf16[384,128]{1,0:T(8,128)(2,1)}, u32[]{:S(2)}) copy-start(bf16[384,128]{1,0:T(8,128)(2,1)} %param.16) | copy-start | bytes 294916
  103.7 212.1 %reduce-scatter.5.cloned.1.call-start = ((), (), s32[]{:S(2)}) async-start(), calls=%async_computation.5 | async-start | bytes 1671168 | tf_op jit(solution)/shard_map/reduce_scatter | solution.py:58
  248.8 69.0 %copy-start.1 = (bf16[535,128]{1,0:T(8,128)(2,1)S(1)}, bf16[535,128]{1,0:T(8,128)(2,1)}, u32[]{:S(2)}) copy-start(bf16[535,128]{1,0:T(8,128)(2,1)} %param.25) | copy-start | bytes 410884
Sparse Core Ops, SparseCore 0:
  103.8 61.9 reduce-scatter.2
  252.7 63.0 reduce-scatter.4
where the time goes:
time: 327 us; the launch traced here: 325 us
  waiting for transfers between devices  173 us (53%)
  blocking collectives  52.9 us (16%)
  local copies, waits for them, and re-layouts  32 us (10%)
  matrix products  27.1 us (8%)
  other arithmetic  15.1 us (5%)
  between operations  13.7 us (4%)
  starting transfers between devices  10.6 us (3%)
    reduce_scatter x2, waiting for transfers between devices, body(): lax.psum_scatter(partial_sum.reshape(group_blocks * size_block, width).as...  125 us
    all_to_all x1, blocking collectives, body(): lax.all_to_all(picked, 'node', split_axis=0, concat_axis=0, tiled=True)  52.9 us
    all_to_all x1, waiting for transfers between devices, body(): lax.all_to_all(picked, 'node', split_axis=0, concat_axis=0, tiled=True)  48.5 us
    dot_general x2, local copies, waits for them, and re-layouts, body(): jnp.einsum('tij,tjf->tif', adjacency, modulated, preferred_element_type=j...  18.8 us
    dot_general x2, matrix products, body(): jnp.einsum('tij,tjf->tif', adjacency, modulated, preferred_element_type=j...  18.4 us
    all_to_all x1, starting transfers between devices, body(): lax.all_to_all(picked, 'node', split_axis=0, concat_axis=0, tiled=True)  10.5 us
    convert_element_type x2, other arithmetic, body(): (flat_products - high_part.astype(jnp.float32)).astype(jnp.bfloat16)  8.06 us
  transfers between devices with their start and end apart: 3, of which 3 were waited for; matrix products, arithmetic and copies ran while one was open for 0% of the time, Pallas kernels for 0%

commit v1 on v0

v1 whole, which is shorter than its diff:
```python
import jax
import jax.numpy as jnp
import numpy as np
from jax import lax
from jax.sharding import Mesh
from jax.sharding import PartitionSpec as P

NODE_AXES = ("x", "y")
TILE_AXES = ("z", "core")
ALL_AXES = NODE_AXES + TILE_AXES


def body(
    states,
    adjacency,
    tile_node,
    tile_block,
    tile_rel,
    tile_dst,
    send_blocks,
    send_count,
    active,
    relations,
    mix_weight,
    norm_gain,
):
    size_block = adjacency.shape[1]
    width = states.shape[1]
    own_blocks = states.shape[0] // size_block
    n_z = lax.axis_size("z")
    n_core = lax.axis_size("core")
    group_blocks = own_blocks * n_z * n_core
    tiles_here = adjacency.shape[0]
    depth = mix_weight.shape[1]
    query_count = width // depth
    me_node = lax.axis_index("x") * lax.axis_size("y") + lax.axis_index("y")

    lists_all = lax.all_gather(send_blocks[0], NODE_AXES, axis=0, tiled=False)
    counts_all = lax.all_gather(send_count[0], NODE_AXES, axis=0, tiled=False)
    lists_mine = lax.dynamic_index_in_dim(lists_all, me_node, axis=1, keepdims=False)
    counts_mine = lax.dynamic_index_in_dim(counts_all, me_node, axis=1, keepdims=False)
    sender = tile_node[0]
    slot = tile_block[0]
    local_block = jnp.clip(lists_mine[sender, slot], 0, own_blocks - 1)
    valid = (slot < counts_mine[sender]).astype(jnp.float32)
    source_index = sender * own_blocks + local_block

    rel_onehot = (
        tile_rel[0][:, None] == jnp.arange(relations.shape[0], dtype=jnp.int32)[None, :]
    ).astype(jnp.bfloat16)
    rel_rows = jnp.dot(rel_onehot, relations, preferred_element_type=jnp.float32)
    rel_rows = rel_rows * valid[:, None]
    dst_onehot = (
        jnp.arange(group_blocks, dtype=jnp.int32)[:, None] == tile_dst[0][None, :]
    ).astype(jnp.bfloat16)
    for layer in range(mix_weight.shape[0]):
        blocks = states.reshape(own_blocks, size_block, width) * active[layer][
            :, None, None
        ].astype(jnp.bfloat16)
        gathered = lax.all_gather(blocks, NODE_AXES, axis=0, tiled=True)
        source_rows = jnp.take(gathered, source_index, axis=0)
        modulated = (source_rows * rel_rows[:, None, :]).astype(jnp.bfloat16)
        products = jnp.einsum(
            "tij,tjf->tif", adjacency, modulated, preferred_element_type=jnp.float32
        )
        flat_products = products.reshape(tiles_here, -1)
        high_part = flat_products.astype(jnp.bfloat16)
        low_part = (flat_products - high_part.astype(jnp.float32)).astype(jnp.bfloat16)
        partial_sum = jnp.dot(dst_onehot, high_part, preferred_element_type=jnp.float32) + jnp.dot(
            dst_onehot, low_part, preferred_element_type=jnp.float32
        )
        partial_sum = partial_sum.astype(jnp.bfloat16).reshape(
            n_z, n_core, own_blocks * size_block, width
        )
        by_core = jnp.swapaxes(partial_sum, 0, 1).reshape(-1, width)
        half = lax.psum_scatter(by_core, "core", scatter_dimension=0, tiled=True)
        summed = lax.psum_scatter(half, "z", scatter_dimension=0, tiled=True)
        mixer = jnp.kron(jnp.eye(query_count, dtype=jnp.bfloat16), mix_weight[layer])
        mixed = jnp.dot(summed, mixer, preferred_element_type=jnp.float32).reshape(
            -1, query_count, depth
        )
        center = jnp.mean(mixed, axis=-1, keepdims=True)
        spread = jnp.mean(jnp.square(mixed - center), axis=-1, keepdims=True)
        normed = (mixed - center) * lax.rsqrt(spread + 1e-05) * norm_gain[layer]
        states = (states.astype(jnp.float32) + jax.nn.relu(normed).reshape(-1, width)).astype(
            jnp.bfloat16
        )
    return states


def solution(mesh):
    n_node, n_tile = mesh.devices.shape
    n_x = 4 if n_node % 4 == 0 else 1
    n_y = n_node // n_x
    fine = Mesh(np.asarray(mesh.devices).reshape(n_x, n_y, n_tile // 2, 2), ALL_AXES)
    rows = P(ALL_AXES, None)
    placed = (
        rows,
        P(ALL_AXES, None, None),
        rows,
        rows,
        rows,
        rows,
        P(ALL_AXES, None, None),
        rows,
        P(None, ALL_AXES),
        P(),
        P(),
        P(),
    )
    return jax.shard_map(body, mesh=fine, in_specs=placed, out_specs=rows, check_vma=False)
```

time: 327 us -> 381 us (1.17)
  waiting for transfers between devices: 173 us -> 223 us
  starting transfers between devices: 10.6 us -> 0.39 us
  blocking collectives: 52.9 us -> 60.8 us
  local copies, waits for them, and re-layouts: 32 us -> 36.9 us
    all_gather x0 -> x2, waiting for transfers between devices: none -> 105 us  [body(): gathered = lax.all_gather(blocks, NODE_AXES, axis=0, tiled=True)]
    all_gather x0 -> x2, blocking collectives: none -> 60.8 us  [the longest x1 33.8 us: body(): lists_all = lax.all_gather(send_blocks[0], NODE_AXES, axis=0, tiled=False)]
    all_to_all x1 -> x0, blocking collectives: 52.9 us -> none  [body(): lax.all_to_all(picked, 'node', split_axis=0, concat_axis=0, tiled=True)]
    all_to_all x1 -> x0, waiting for transfers between devices: 48.5 us -> none  [body(): lax.all_to_all(picked, 'node', split_axis=0, concat_axis=0, tiled=True)]
    all_to_all x1 -> x0, starting transfers between devices: 10.5 us -> none  [body(): lax.all_to_all(picked, 'node', split_axis=0, concat_axis=0, tiled=True)]
    reduce_scatter x2 -> x4, waiting for transfers between devices: 125 us -> 118 us  [the longest x2 78.8 us: body(): summed = lax.psum_scatter(half, 'z', scatter_dimension=0, tiled=True)]
    gather x4, local copies, waits for them, and re-layouts: 7.98 us -> 12.6 us  [the longest x2 9.87 us: body(): source_rows = jnp.take(gathered, source_index, axis=0)]
    convert_element_type x2 -> x0, local copies, waits for them, and re-layouts: 4.23 us -> none  [body(): partial_sum.reshape(group_blocks * size_block, width).astype(jnp.bfloat16)]
  transfers between devices with their start and end apart: 3 -> 6, of which waited for: 3 -> 6; matrix products, arithmetic and copies ran while one was open for 0% -> 2% of each run, Pallas kernels for 0% -> 0%
where the time goes in v1:
time: 381 us; the launch traced here: 377 us
  waiting for transfers between devices  223 us (59%)
  blocking collectives  60.8 us (16%)
  local copies, waits for them, and re-layouts  36.9 us (10%)
  matrix products  27.7 us (7%)
  other arithmetic  14.3 us (4%)
  between operations  13.8 us (4%)
    all_gather x2, waiting for transfers between devices, body(): gathered = lax.all_gather(blocks, NODE_AXES, axis=0, tiled=True)  105 us
    reduce_scatter x2, waiting for transfers between devices, body(): summed = lax.psum_scatter(half, 'z', scatter_dimension=0, tiled=True)  78.8 us
    reduce_scatter x2, waiting for transfers between devices, body(): half = lax.psum_scatter(by_core, 'core', scatter_dimension=0, tiled=True)  38.9 us
    all_gather x1, blocking collectives, body(): lists_all = lax.all_gather(send_blocks[0], NODE_AXES, axis=0, tiled=False)  33.8 us
    all_gather x1, blocking collectives, body(): counts_all = lax.all_gather(send_count[0], NODE_AXES, axis=0, tiled=False)  27 us
    dot_general x2, local copies, waits for them, and re-layouts, body(): jnp.einsum('tij,tjf->tif', adjacency, modulated, preferred_element_type=j...  18.6 us
    dot_general x2, matrix products, body(): jnp.einsum('tij,tjf->tif', adjacency, modulated, preferred_element_type=j...  18.5 us
    gather x2, local copies, waits for them, and re-layouts, body(): source_rows = jnp.take(gathered, source_index, axis=0)  9.87 us
  transfers between devices with their start and end apart: 6, of which 6 were waited for; matrix products, arithmetic and copies ran while one was open for 2% of the time, Pallas kernels for 0%

profile of v1, /device:TPU:1, one launch (start us, length us, event | category | flops | bytes accessed | tf_op | source)
XLA Modules:
  0.0 376.7 jit_solution(17460445903867488199)
XLA Ops:
  7.3 1.6 broadcast_multiply_fusion.1
  9.0 33.8 %all_gather.13 = s32[32,32,2]{1,2,0:T(2,128)S(1)} all-gather(s32[1,32,2]{1,2,0:T(2,128)} %param.20), channel_id=1, replica_groups=mesh['x'=4,'y'=8,'z'=8,'core'=2] {'x','y'}, dimensions={0}, use_global_device_ids=true | all-gather | bytes 8448 | tf_op jit(solution)/shard_map/all_gather | solution.py:38
  43.6 1.5 gather_fusion
  45.1 27.0 %all-gather = s32[32,1,32]{2,1,0:T(1,128)S(1)} all-gather(s32[1,1,32]{2,1,0:T(1,128)} %bitcast.105), channel_id=1, replica_groups=mesh['x'=4,'y'=8,'z'=8,'core'=2] {'x','y'}, dimensions={0}, use_global_device_ids=true | all-gather | bytes 4224 | tf_op jit(solution)/shard_map/all_gather | solution.py:39
  76.3 20.6 %all-gather.4.cloned.1.call-done = bf16[96,128,128]{2,1,0:T(8,128)(2,1)} async-done(((bf16[3,128,128]{2,1,0:T(8,128)(2,1)}), bf16[96,128,128]{2,1,0:T(8,128)(2,1)}) %all-gather.4.cloned.1.call-update) | async-done | bytes 3145744 | tf_op jit(solution)/shard_map/all_gather | solution.py:60
  96.9 4.9 %gather_fusion.2 = bf16[128,128,128]{2,1,0:T(8,128)(2,1)} fusion(bf16[96,128,128]{2,1,0:T(8,128)(2,1)} %all-gather.4.cloned.1.call-done, s32[1024]{0:T(1024)S(1)} %pad_clamp_fusion.1), kind=kCustom, calls=%fused_computation.clone | custom fusion | bytes 8389120 | tf_op jit(solution)/shard_map/jit(_take)/gather | solution.py:61
  101.8 9.2 %fusion.13 = f32[128,128,128]{1,2,0:T(8,128)} fusion(bf16[128,128,128]{2,1,0:T(8,128)(2,1)} %param.15, bf16[128,128,128]{2,1,0:T(8,128)(2,1)} %gather_fusion.2, f32[128,128]{1,0:T(8,128)S(1)} %convolution_multiply_fusion, pred[128]{0:T(512)(128)(4,1)S(1)} %get-tuple-element.10), kind=kOutput, calls=%fused_computation.25 | convolution fusion | flops 545259520 | bytes 16842880 | tf_op jit(solution)/shard_map/tij,tjf->tif/dot_general | solution.py:63
  111.1 9.3 %copy.33 = f32[128,128,128]{0,2,1:T(8,128)} copy(f32[128,128,128]{1,2,0:T(8,128)} %fusion.13) | data formatting | bytes 16777216 | tf_op jit(solution)/shard_map/tij,tjf->tif/dot_general | solution.py:63
  120.4 4.0 %fusion.3 = (bf16[128,16384]{0,1:T(8,128)(2,1)S(1)}, bf16[128,16384]{0,1:T(8,128)(2,1)S(1)}) fusion(f32[128,128,128]{0,2,1:T(8,128)} %copy.33), kind=kLoop, calls=%fused_computation.13 | loop fusion | flops 8388608 | bytes 16777216 | tf_op jit(solution)/shard_map/convert_element_type | solution.py:68
  124.4 1.5 fusion.22
  126.0 1.5 fusion
  128.4 1.3 copy.34
  129.7 19.4 %reduce-scatter.5.cloned.1.call-done = bf16[3072,128]{1,0:T(8,128)(2,1)} async-done(((bf16[6144,128]{1,0:T(8,128)(2,1)}), bf16[3072,128]{1,0:T(8,128)(2,1)}) %reduce-scatter.5.cloned.1.call-update) | async-done | bytes 786448 | tf_op jit(solution)/shard_map/reduce_scatter | solution.py:76
  149.7 39.2 %reduce-scatter.7.cloned.1.call-done = bf16[384,128]{1,0:T(8,128)(2,1)} async-done(((bf16[3072,128]{1,0:T(8,128)(2,1)}), bf16[384,128]{1,0:T(8,128)(2,1)}) %reduce-scatter.7.cloned.1.call-update) | async-done | bytes 98320 | tf_op jit(solution)/shard_map/reduce_scatter | solution.py:77
  191.3 84.5 %all-gather.6.cloned.1.call-done = bf16[96,128,128]{2,1,0:T(8,128)(2,1)} async-done(((bf16[3,128,128]{2,1,0:T(8,128)(2,1)}), bf16[96,128,128]{2,1,0:T(8,128)(2,1)}) %all-gather.6.cloned.1.call-update) | async-done | bytes 3145744 | tf_op jit(solution)/shard_map/all_gather | solution.py:60
  275.9 4.9 %gather_fusion.3 = bf16[128,128,128]{2,1,0:T(8,128)(2,1)} fusion(bf16[96,128,128]{2,1,0:T(8,128)(2,1)} %all-gather.6.cloned.1.call-done, s32[1024]{0:T(1024)S(1)} %pad_clamp_fusion.1), kind=kCustom, calls=%fused_computation.1.clone | custom fusion | bytes 8389120 | tf_op jit(solution)/shard_map/jit(_take)/gather | solution.py:61
  280.8 9.2 %fusion.12 = f32[128,128,128]{1,2,0:T(8,128)} fusion(bf16[128,128,128]{2,1,0:T(8,128)(2,1)} %param.15, bf16[128,128,128]{2,1,0:T(8,128)(2,1)} %gather_fusion.3, f32[128,128]{1,0:T(8,128)S(1)} %convolution_multiply_fusion, pred[128]{0:T(512)(128)(4,1)S(1)} %get-tuple-element.10), kind=kOutput, calls=%fused_computation.24 | convolution fusion | flops 545259520 | bytes 16842880 | tf_op jit(solution)/shard_map/tij,tjf->tif/dot_general | solution.py:63
  290.1 9.3 %copy.38 = f32[128,128,128]{0,2,1:T(8,128)} copy(f32[128,128,128]{1,2,0:T(8,128)} %fusion.12) | data formatting | bytes 16777216 | tf_op jit(solution)/shard_map/tij,tjf->tif/dot_general | solution.py:63
  299.4 4.0 %fusion.2 = (bf16[128,16384]{0,1:T(8,128)(2,1)S(1)}, bf16[128,16384]{0,1:T(8,128)(2,1)S(1)}) fusion(f32[128,128,128]{0,2,1:T(8,128)} %copy.38), kind=kLoop, calls=%fused_computation.10 | loop fusion | flops 8388608 | bytes 16777216 | tf_op jit(solution)/shard_map/convert_element_type | solution.py:68
  303.4 1.5 fusion.21
  305.0 1.5 fusion.1
  307.3 1.3 copy.39
  308.6 19.5 %reduce-scatter.9.cloned.1.call-done = bf16[3072,128]{1,0:T(8,128)(2,1)} async-done(((bf16[6144,128]{1,0:T(8,128)(2,1)}), bf16[3072,128]{1,0:T(8,128)(2,1)}) %reduce-scatter.9.cloned.1.call-update) | async-done | bytes 786448 | tf_op jit(solution)/shard_map/reduce_scatter | solution.py:76
  328.2 39.5 %reduce-scatter.11.cloned.1.call-done = bf16[384,128]{1,0:T(8,128)(2,1)} async-done(((bf16[3072,128]{1,0:T(8,128)(2,1)}), bf16[384,128]{1,0:T(8,128)(2,1)}) %reduce-scatter.11.cloned.1.call-update) | async-done | bytes 98320 | tf_op jit(solution)/shard_map/reduce_scatter | solution.py:77
  (61 shorter events, 12.6 us)
Async XLA Ops:
  6.5 68.9 %copy-start = (bf16[535,128]{1,0:T(8,128)(2,1)S(1)}, bf16[535,128]{1,0:T(8,128)(2,1)}, u32[]{:S(2)}) copy-start(bf16[535,128]{1,0:T(8,128)(2,1)} %param.23) | copy-start | bytes 410884
  6.5 90.4 %all-gather.4.cloned.1.call-start = ((), (), s32[]{:S(2)}) async-start(), calls=%async_computation.4 | async-start | bytes 3244032 | tf_op jit(solution)/shard_map/all_gather | solution.py:60
  8.9 140.2 %reduce-scatter.5.cloned.1.call-start = ((), (), s32[]{:S(2)}) async-start(), calls=%async_computation.5 | async-start | bytes 2359296 | tf_op jit(solution)/shard_map/reduce_scatter | solution.py:76
  120.4 4.0 %copy-start.4 = (s32[1,128]{1,0:T(1,128)S(1)}, s32[1,128]{1,0:T(1,128)}, u32[]{:S(2)}) copy-start(s32[1,128]{1,0:T(1,128)} %param.19) | copy-start | bytes 1540
  127.5 21.6 %copy-start.3 = (bf16[2,64,64]{2,1,0:T(8,128)(2,1)S(1)}, bf16[2,64,64]{2,1,0:T(8,128)(2,1)}, u32[]{:S(2)}) copy-start(bf16[2,64,64]{2,1,0:T(8,128)(2,1)} %param.24) | copy-start | bytes 49156
  127.6 22.1 %copy-start.5 = (f32[2,64]{1,0:T(2,128)S(1)}, f32[2,64]{1,0:T(2,128)}, u32[]{:S(2)}) copy-start(f32[2,64]{1,0:T(2,128)} %param.25) | copy-start | bytes 1540
  128.4 62.0 %copy-start.2 = (bf16[384,128]{1,0:T(8,128)(2,1)S(1)}, bf16[384,128]{1,0:T(8,128)(2,1)}, u32[]{:S(2)}) copy-start(bf16[384,128]{1,0:T(8,128)(2,1)} %param.14) | copy-start | bytes 294916
  129.6 59.3 %reduce-scatter.7.cloned.1.call-start = ((), (), s32[]{:S(2)}) async-start(), calls=%async_computation.6 | async-start | bytes 884736 | tf_op jit(solution)/shard_map/reduce_scatter | solution.py:77
  149.1 126.8 %all-gather.6.cloned.1.call-start = ((), (), s32[]{:S(2)}) async-start(), calls=%async_computation.7 | async-start | bytes 3244032 | tf_op jit(solution)/shard_map/all_gather | solution.py:60
  191.1 137.0 %reduce-scatter.9.cloned.1.call-start = ((), (), s32[]{:S(2)}) async-start(), calls=%async_computation.8 | async-start | bytes 2359296 | tf_op jit(solution)/shard_map/reduce_scatter | solution.py:76
  306.5 63.3 %copy-start.1 = (bf16[535,128]{1,0:T(8,128)(2,1)S(1)}, bf16[535,128]{1,0:T(8,128)(2,1)}, u32[]{:S(2)}) copy-start(bf16[535,128]{1,0:T(8,128)(2,1)} %param.23) | copy-start | bytes 410884
  308.6 59.2 %reduce-scatter.11.cloned.1.call-start = ((), (), s32[]{:S(2)}) async-start(), calls=%async_computation.9 | async-start | bytes 884736 | tf_op jit(solution)/shard_map/reduce_scatter | solution.py:77
Sparse Core Ops, SparseCore 0:
  10.5 86.3 all-gather.3
  129.8 19.2 reduce-scatter.4
  151.9 36.9 reduce-scatter.6
  192.0 83.8 all-gather.5
  308.7 19.3 reduce-scatter.8
  330.8 36.9 reduce-scatter.10

commit v2 on v0

--- a/solution.py
+++ b/solution.py
@@ -54,13 +54,11 @@
         partial_sum = jnp.dot(dst_onehot, high_part, preferred_element_type=jnp.float32) + jnp.dot(
             dst_onehot, low_part, preferred_element_type=jnp.float32
         )
-        partial_sum = lax.optimization_barrier(partial_sum.astype(jnp.bfloat16)).astype(jnp.float32)
-        summed = lax.psum_scatter(
-            partial_sum.reshape(group_blocks * size_block, width).astype(jnp.bfloat16),
-            "tile",
-            scatter_dimension=0,
-            tiled=True,
+        partial_sum = partial_sum.astype(jnp.bfloat16).reshape(
+            lax.axis_size("tile"), own_blocks * size_block, width
         )
+        received = lax.all_to_all(partial_sum, "tile", split_axis=0, concat_axis=0, tiled=True)
+        summed = jnp.sum(received.astype(jnp.float32), axis=0).astype(jnp.bfloat16)
         mixer = jnp.kron(jnp.eye(query_count, dtype=jnp.bfloat16), mix_weight[layer])
         mixed = jnp.dot(summed, mixer, preferred_element_type=jnp.float32).reshape(
             -1, query_count, depth

time: 327 us -> 283 us (0.87)
  waiting for transfers between devices: 173 us -> 125 us
  starting transfers between devices: 10.6 us -> 28.4 us
  between operations: 13.7 us -> 0.35 us
    reduce_scatter x2 -> x0, waiting for transfers between devices: 125 us -> none  [body(): lax.psum_scatter(partial_sum.reshape(group_blocks * size_block, width).as...]
    all_to_all x0 -> x2, waiting for transfers between devices: none -> 76.4 us  [body(): lax.all_to_all(partial_sum, 'tile', split_axis=0, concat_axis=0, tiled=True)]
    all_to_all x0 -> x2, starting transfers between devices: none -> 17.9 us  [body(): lax.all_to_all(partial_sum, 'tile', split_axis=0, concat_axis=0, tiled=True)]
    convert_element_type x2 -> x0, local copies, waits for them, and re-layouts: 4.23 us -> none  [body(): partial_sum.reshape(group_blocks * size_block, width).astype(jnp.bfloat16)]
    reshape x0 -> x2, local copies, waits for them, and re-layouts: none -> 4.2 us  [body(): partial_sum.astype(jnp.bfloat16)]
where the time goes in v2:
time: 283 us; the launch traced here: 282 us
  waiting for transfers between devices  125 us (44%)
  blocking collectives  55.9 us (20%)
  local copies, waits for them, and re-layouts  31.9 us (11%)
  starting transfers between devices  28.4 us (10%)
  matrix products  25.3 us (9%)
  other arithmetic  15.5 us (5%)
    all_to_all x2, waiting for transfers between devices, body(): lax.all_to_all(partial_sum, 'tile', split_axis=0, concat_axis=0, tiled=True)  76.4 us
    all_to_all x1, blocking collectives, body(): lax.all_to_all(picked, 'node', split_axis=0, concat_axis=0, tiled=True)  55.9 us
    all_to_all x1, waiting for transfers between devices, body(): lax.all_to_all(picked, 'node', split_axis=0, concat_axis=0, tiled=True)  48.6 us
    dot_general x2, local copies, waits for them, and re-layouts, body(): jnp.einsum('tij,tjf->tif', adjacency, modulated, preferred_element_type=j...  18.7 us
    dot_general x2, matrix products, body(): jnp.einsum('tij,tjf->tif', adjacency, modulated, preferred_element_type=j...  18.4 us
    all_to_all x2, starting transfers between devices, body(): lax.all_to_all(partial_sum, 'tile', split_axis=0, concat_axis=0, tiled=True)  17.9 us
    all_to_all x1, starting transfers between devices, body(): lax.all_to_all(picked, 'node', split_axis=0, concat_axis=0, tiled=True)  10.5 us
    convert_element_type x2, other arithmetic, body(): (flat_products - high_part.astype(jnp.float32)).astype(jnp.bfloat16)  8.06 us
  transfers between devices with their start and end apart: 3, of which 3 were waited for; matrix products, arithmetic and copies ran while one was open for 0% of the time, Pallas kernels for 0%

profile of v2, /device:TPU:1, one launch (start us, length us, event | category | flops | bytes accessed | tf_op | source)
XLA Modules:
  0.0 282.3 jit_solution(3195503404707720623)
XLA Ops:
  3.1 1.0 broadcast_multiply_fusion.1
  4.1 0.9 gather_fusion
  5.1 1.7 select_select_fusion.1
  6.8 10.5 %all-to-all-start = ((bf16[32,2,128,128]{3,2,1,0:T(8,128)(2,1)}), bf16[32,2,128,128]{3,2,1,0:T(8,128)(2,1)S(1)}, u32[]{:S(2)}, u32[]{:S(2)}) async-start(bf16[32,2,128,128]{3,2,1,0:T(8,128)(2,1)} %select_select_fusion.1), calls=%async_computation | async-start | bytes 4194304 | tf_op jit(solution)/shard_map/all_to_all | solution.py:43
  17.6 48.6 %all-to-all-done = bf16[32,2,128,128]{3,2,1,0:T(8,128)(2,1)S(1)} async-done(((bf16[32,2,128,128]{3,2,1,0:T(8,128)(2,1)}), bf16[32,2,128,128]{3,2,1,0:T(8,128)(2,1)S(1)}, u32[]{:S(2)}, u32[]{:S(2)}) %all-to-all-start) | async-done | bytes 2097184 | tf_op jit(solution)/shard_map/all_to_all | solution.py:43
  66.2 3.1 %gather_fusion.1 = bf16[128,128,128]{2,1,0:T(8,128)(2,1)} fusion(bf16[64,128,128]{2,1,0:T(8,128)(2,1)S(1)} %bitcast.75, s32[1024]{0:T(1024)S(1)} %pad_clamp_fusion), kind=kCustom, calls=%fused_computation.1.clone | custom fusion | bytes 8389120 | tf_op jit(solution)/shard_map/jit(_take)/gather | solution.py:46
  69.2 9.2 %fusion.13 = f32[128,128,128]{1,2,0:T(8,128)} fusion(bf16[128,128,128]{2,1,0:T(8,128)(2,1)} %param.17, bf16[128,128,128]{2,1,0:T(8,128)(2,1)} %gather_fusion.1, f32[128,128]{1,0:T(8,128)S(1)} %fusion.16, pred[128]{0:T(512)(128)(4,1)S(1)} %get-tuple-element.11), kind=kOutput, calls=%fused_computation.25 | convolution fusion | flops 545259520 | bytes 16842880 | tf_op jit(solution)/shard_map/tij,tjf->tif/dot_general | solution.py:48
  78.4 9.3 %copy.24 = f32[128,128,128]{0,2,1:T(8,128)} copy(f32[128,128,128]{1,2,0:T(8,128)} %fusion.13) | data formatting | bytes 16777216 | tf_op jit(solution)/shard_map/tij,tjf->tif/dot_general | solution.py:48
  87.8 4.0 %fusion.3 = (bf16[128,16384]{0,1:T(8,128)(2,1)S(1)}, bf16[128,16384]{0,1:T(8,128)(2,1)S(1)}) fusion(f32[128,128,128]{0,2,1:T(8,128)} %copy.24), kind=kLoop, calls=%fused_computation.13 | loop fusion | flops 8388608 | bytes 16777216 | tf_op jit(solution)/shard_map/convert_element_type | solution.py:53
  91.8 1.5 fusion.23
  93.4 1.5 fusion
  95.0 2.1 reshape.139
  97.1 12.4 %all-to-all-start.1 = ((bf16[16,384,128]{2,1,0:T(8,128)(2,1)}), bf16[16,384,128]{2,1,0:T(8,128)(2,1)S(1)}, u32[]{:S(2)}, u32[]{:S(2)}) async-start(bf16[16,384,128]{2,1,0:T(8,128)(2,1)} %reshape.139), calls=%async_computation.1 | async-start | bytes 3145728 | tf_op jit(solution)/shard_map/all_to_all | solution.py:60
  110.0 38.0 %all-to-all-done.1 = bf16[16,384,128]{2,1,0:T(8,128)(2,1)S(1)} async-done(((bf16[16,384,128]{2,1,0:T(8,128)(2,1)}), bf16[16,384,128]{2,1,0:T(8,128)(2,1)S(1)}, u32[]{:S(2)}, u32[]{:S(2)}) %all-to-all-start.1) | async-done | bytes 1572896 | tf_op jit(solution)/shard_map/all_to_all | solution.py:60
  150.2 55.9 %all_to_all.20 = bf16[32,2,128,128]{3,2,1,0:T(8,128)(2,1)S(1)} all-to-all(bf16[32,2,128,128]{3,2,1,0:T(8,128)(2,1)S(1)} %select_select_fusion), channel_id=1, replica_groups=mesh['node'=32,'tile'=16] {'node'}, dimensions={0} | all-to-all | bytes 4194304 | tf_op jit(solution)/shard_map/all_to_all | solution.py:43
  206.1 3.1 %gather_fusion.3 = bf16[128,128,128]{2,1,0:T(8,128)(2,1)} fusion(bf16[64,128,128]{2,1,0:T(8,128)(2,1)S(1)} %bitcast.76, s32[1024]{0:T(1024)S(1)} %pad_clamp_fusion), kind=kCustom, calls=%fused_computation.3.clone | custom fusion | bytes 8389120 | tf_op jit(solution)/shard_map/jit(_take)/gather | solution.py:46
  209.1 9.2 %fusion.12 = f32[128,128,128]{1,2,0:T(8,128)} fusion(bf16[128,128,128]{2,1,0:T(8,128)(2,1)} %param.17, bf16[128,128,128]{2,1,0:T(8,128)(2,1)} %gather_fusion.3, f32[128,128]{1,0:T(8,128)S(1)} %fusion.16, pred[128]{0:T(512)(128)(4,1)S(1)} %get-tuple-element.11), kind=kOutput, calls=%fused_computation.24 | convolution fusion | flops 545259520 | bytes 16842880 | tf_op jit(solution)/shard_map/tij,tjf->tif/dot_general | solution.py:48
  218.3 9.3 %copy.30 = f32[128,128,128]{0,2,1:T(8,128)} copy(f32[128,128,128]{1,2,0:T(8,128)} %fusion.12) | data formatting | bytes 16777216 | tf_op jit(solution)/shard_map/tij,tjf->tif/dot_general | solution.py:48
  227.7 4.0 %fusion.2 = (bf16[128,16384]{0,1:T(8,128)(2,1)S(1)}, bf16[128,16384]{0,1:T(8,128)(2,1)S(1)}) fusion(f32[128,128,128]{0,2,1:T(8,128)} %copy.30), kind=kLoop, calls=%fused_computation.10 | loop fusion | flops 8388608 | bytes 16777216 | tf_op jit(solution)/shard_map/convert_element_type | solution.py:53
  231.7 1.5 fusion.22
  233.3 1.5 fusion.1
  234.8 2.1 reshape.144
  236.9 5.5 %all-to-all-start.3 = ((bf16[16,384,128]{2,1,0:T(8,128)(2,1)}), bf16[16,384,128]{2,1,0:T(8,128)(2,1)S(1)}, u32[]{:S(2)}, u32[]{:S(2)}) async-start(bf16[16,384,128]{2,1,0:T(8,128)(2,1)} %reshape.144), calls=%async_computation.3 | async-start | bytes 3145728 | tf_op jit(solution)/shard_map/all_to_all | solution.py:60
  242.5 38.4 %all-to-all-done.3 = bf16[16,384,128]{2,1,0:T(8,128)(2,1)S(1)} async-done(((bf16[16,384,128]{2,1,0:T(8,128)(2,1)}), bf16[16,384,128]{2,1,0:T(8,128)(2,1)S(1)}, u32[]{:S(2)}, u32[]{:S(2)}) %all-to-all-start.3) | async-done | bytes 1572896 | tf_op jit(solution)/shard_map/all_to_all | solution.py:60
  (57 shorter events, 7.4 us)
Async XLA Ops:
  0.0 17.3 %copy-start = (bf16[535,128]{1,0:T(8,128)(2,1)S(1)}, bf16[535,128]{1,0:T(8,128)(2,1)}, u32[]{:S(2)}) copy-start(bf16[535,128]{1,0:T(8,128)(2,1)} %param.25) | copy-start | bytes 410884
  5.1 12.2 %copy-start.6 = (s32[1,128]{1,0:T(1,128)S(1)}, s32[1,128]{1,0:T(1,128)}, u32[]{:S(2)}) copy-start(s32[1,128]{1,0:T(1,128)} %param.19) | copy-start | bytes 1540
  5.1 12.2 %copy-start.7 = (s32[1,128]{1,0:T(1,128)S(1)}, s32[1,128]{1,0:T(1,128)}, u32[]{:S(2)}) copy-start(s32[1,128]{1,0:T(1,128)} %param.18) | copy-start | bytes 1540
  5.1 12.3 %copy-start.8 = (s32[1,128]{1,0:T(1,128)S(1)}, s32[1,128]{1,0:T(1,128)}, u32[]{:S(2)}) copy-start(s32[1,128]{1,0:T(1,128)} %param.20) | copy-start | bytes 1540
  6.8 59.4 %all-to-all-start = ((bf16[32,2,128,128]{3,2,1,0:T(8,128)(2,1)}), bf16[32,2,128,128]{3,2,1,0:T(8,128)(2,1)S(1)}, u32[]{:S(2)}, u32[]{:S(2)}) async-start(bf16[32,2,128,128]{3,2,1,0:T(8,128)(2,1)} %select_select_fusion.1), calls=%async_computation | async-start | bytes 4194304 | tf_op jit(solution)/shard_map/all_to_all | solution.py:43
  87.8 4.0 %copy-start.4 = (s32[1,128]{1,0:T(1,128)S(1)}, s32[1,128]{1,0:T(1,128)}, u32[]{:S(2)}) copy-start(s32[1,128]{1,0:T(1,128)} %param.21) | copy-start | bytes 1540
  94.9 14.6 %copy-start.3 = (bf16[2,64,64]{2,1,0:T(8,128)(2,1)S(1)}, bf16[2,64,64]{2,1,0:T(8,128)(2,1)}, u32[]{:S(2)}) copy-start(bf16[2,64,64]{2,1,0:T(8,128)(2,1)} %param.26) | copy-start | bytes 49156
  95.0 15.1 %copy-start.5 = (f32[2,64]{1,0:T(2,128)S(1)}, f32[2,64]{1,0:T(2,128)}, u32[]{:S(2)}) copy-start(f32[2,64]{1,0:T(2,128)} %param.27) | copy-start | bytes 1540
  95.0 53.8 %copy-start.2 = (bf16[384,128]{1,0:T(8,128)(2,1)S(1)}, bf16[384,128]{1,0:T(8,128)(2,1)}, u32[]{:S(2)}) copy-start(bf16[384,128]{1,0:T(8,128)(2,1)} %param.16) | copy-start | bytes 294916
  97.1 50.9 %all-to-all-start.1 = ((bf16[16,384,128]{2,1,0:T(8,128)(2,1)}), bf16[16,384,128]{2,1,0:T(8,128)(2,1)S(1)}, u32[]{:S(2)}, u32[]{:S(2)}) async-start(bf16[16,384,128]{2,1,0:T(8,128)(2,1)} %reshape.139), calls=%async_computation.1 | async-start | bytes 3145728 | tf_op jit(solution)/shard_map/all_to_all | solution.py:60
  233.3 49.1 %copy-start.1 = (bf16[535,128]{1,0:T(8,128)(2,1)S(1)}, bf16[535,128]{1,0:T(8,128)(2,1)}, u32[]{:S(2)}) copy-start(bf16[535,128]{1,0:T(8,128)(2,1)} %param.25) | copy-start | bytes 410884
  236.9 44.0 %all-to-all-start.3 = ((bf16[16,384,128]{2,1,0:T(8,128)(2,1)}), bf16[16,384,128]{2,1,0:T(8,128)(2,1)S(1)}, u32[]{:S(2)}, u32[]{:S(2)}) async-start(bf16[16,384,128]{2,1,0:T(8,128)(2,1)} %reshape.144), calls=%async_computation.3 | async-start | bytes 3145728 | tf_op jit(solution)/shard_map/all_to_all | solution.py:60

commit v3 on v2

--- a/solution.py
+++ b/solution.py
@@ -21,11 +21,13 @@
     size_block = adjacency.shape[1]
     width = states.shape[1]
     own_blocks = states.shape[0] // size_block
-    group_blocks = own_blocks * lax.axis_size("tile")
+    n_tile = lax.axis_size("tile")
+    group_blocks = own_blocks * n_tile
     tiles_here = adjacency.shape[0]
     capacity = send_blocks.shape[2]
     depth = mix_weight.shape[1]
     query_count = width // depth
+    lanes = 128
     rel_onehot = (
         tile_rel[0][:, None] == jnp.arange(relations.shape[0], dtype=jnp.int32)[None, :]
     ).astype(jnp.bfloat16)
@@ -33,18 +35,21 @@
     dst_onehot = (
         jnp.arange(group_blocks, dtype=jnp.int32)[:, None] == tile_dst[0][None, :]
     ).astype(jnp.bfloat16)
-    for layer in range(mix_weight.shape[0]):
-        blocks = states.reshape(own_blocks, size_block, width) * active[layer][
+    usable = jnp.arange(capacity, dtype=jnp.int32)[None, :] < send_count[0][:, None]
+    slot_index = tile_node[0] * capacity + tile_block[0]
+
+    def one_layer(h, layer, rel_part):
+        blocks = h.reshape(own_blocks, size_block, depth) * active[layer][
             :, None, None
         ].astype(jnp.bfloat16)
-        usable = jnp.arange(capacity, dtype=jnp.int32)[None, :] < send_count[0][:, None]
         picked = jnp.take(blocks, send_blocks[0], axis=0)
         picked = jnp.where(usable[:, :, None, None], picked, jnp.zeros_like(picked))
+        lead = picked.shape[:2]
+        picked = picked.reshape(lead + (size_block * depth // lanes, lanes))
         arrived = lax.all_to_all(picked, "node", split_axis=0, concat_axis=0, tiled=True)
-        slot_index = tile_node[0] * capacity + tile_block[0]
-        source = arrived.reshape(-1, size_block, width)
+        source = arrived.reshape(-1, size_block, depth)
         source_rows = jnp.take(source, slot_index, axis=0)
-        modulated = (source_rows * rel_rows[:, None, :]).astype(jnp.bfloat16)
+        modulated = (source_rows * rel_part[:, None, :]).astype(jnp.bfloat16)
         products = jnp.einsum(
             "tij,tjf->tif", adjacency, modulated, preferred_element_type=jnp.float32
         )
@@ -55,21 +60,26 @@
             dst_onehot, low_part, preferred_element_type=jnp.float32
         )
         partial_sum = partial_sum.astype(jnp.bfloat16).reshape(
-            lax.axis_size("tile"), own_blocks * size_block, width
+            n_tile, own_blocks * size_block * depth // lanes, lanes
         )
         received = lax.all_to_all(partial_sum, "tile", split_axis=0, concat_axis=0, tiled=True)
         summed = jnp.sum(received.astype(jnp.float32), axis=0).astype(jnp.bfloat16)
-        mixer = jnp.kron(jnp.eye(query_count, dtype=jnp.bfloat16), mix_weight[layer])
-        mixed = jnp.dot(summed, mixer, preferred_element_type=jnp.float32).reshape(
-            -1, query_count, depth
-        )
+        summed = summed.reshape(own_blocks * size_block, depth)
+        mixed = jnp.dot(summed, mix_weight[layer], preferred_element_type=jnp.float32)
         center = jnp.mean(mixed, axis=-1, keepdims=True)
         spread = jnp.mean(jnp.square(mixed - center), axis=-1, keepdims=True)
         normed = (mixed - center) * lax.rsqrt(spread + 1e-05) * norm_gain[layer]
-        states = (states.astype(jnp.float32) + jax.nn.relu(normed).reshape(-1, width)).astype(
-            jnp.bfloat16
-        )
-    return states
+        return (h.astype(jnp.float32) + jax.nn.relu(normed)).astype(jnp.bfloat16)
+
+    halves = []
+    for query in range(query_count):
+        columns = slice(query * depth, (query + 1) * depth)
+        h = states[:, columns]
+        rel_part = rel_rows[:, columns]
+        for layer in range(mix_weight.shape[0]):
+            h = one_layer(h, layer, rel_part)
+        halves.append(h)
+    return jnp.concatenate(halves, axis=1)
 
 
 def solution(mesh):

time: 283 us -> 311 us (1.099)
  blocking collectives: 55.9 us -> 0 us
  local copies, waits for them, and re-layouts: 31.9 us -> 65.8 us
  starting transfers between devices: 28.4 us -> 57.4 us
  other arithmetic: 15.5 us -> 25.2 us
  matrix products: 25.3 us -> 32.3 us
    all_to_all x1 -> x0, blocking collectives: 55.9 us -> none  [body(): lax.all_to_all(picked, 'node', split_axis=0, concat_axis=0, tiled=True)]
    all_to_all x3 -> x8, starting transfers between devices: 28.4 us -> 57.4 us  [the longest x4 31.8 us: one_layer(): lax.all_to_all(partial_sum, 'tile', split_axis=0, concat_axis=0, tiled=True)]
    reshape x4 -> x20, local copies, waits for them, and re-layouts: 4.44 us -> 28 us  [the longest x4 13.6 us: one_layer(): picked = picked.reshape(lead + (size_block * depth // lanes, lanes))]
    dot_general x8 -> x16, matrix products: 25 us -> 32 us  [the longest x4 24.4 us: one_layer(): jnp.einsum('tij,tjf->tif', adjacency, modulated, preferred_element_type=j...]
    select_n x3 -> x4, other arithmetic: 2.73 us -> 7.65 us  [the longest x3 6.93 us: one_layer(): picked = jnp.where(usable[:, :, None, None], picked, jnp.zeros_like(picked))]
    gather x4 -> x12, local copies, waits for them, and re-layouts: 8 us -> 12.2 us  [the longest x8 7.99 us: one_layer(): picked = jnp.take(blocks, send_blocks[0], axis=0)]
    reduce_sum x4 -> x8, other arithmetic: 0.51 us -> 4.01 us  [the longest x4 3.89 us: one_layer(): summed = jnp.sum(received.astype(jnp.float32), axis=0).astype(jnp.bfloat16)]
    dot_general x2 -> x4, local copies, waits for them, and re-layouts: 18.7 us -> 21.9 us  [one_layer(): jnp.einsum('tij,tjf->tif', adjacency, modulated, preferred_element_type=j...]
  transfers between devices with their start and end apart: 3 -> 8, of which waited for: 3 -> 8; matrix products, arithmetic and copies ran while one was open for 0% -> 22% of each run, Pallas kernels for 0% -> 0%
where the time goes in v3:
time: 311 us; the launch traced here: 309 us
  waiting for transfers between devices  128 us (41%)
  local copies, waits for them, and re-layouts  65.8 us (21%)
  starting transfers between devices  57.4 us (18%)
  matrix products  32.3 us (10%)
  other arithmetic  25.2 us (8%)
    all_to_all x4, waiting for transfers between devices, one_layer(): lax.all_to_all(picked, 'node', split_axis=0, concat_axis=0, tiled=True)  77.3 us
    all_to_all x4, waiting for transfers between devices, one_layer(): lax.all_to_all(partial_sum, 'tile', split_axis=0, concat_axis=0, tiled=True)  50.6 us
    all_to_all x4, starting transfers between devices, one_layer(): lax.all_to_all(partial_sum, 'tile', split_axis=0, concat_axis=0, tiled=True)  31.8 us
    all_to_all x4, starting transfers between devices, one_layer(): lax.all_to_all(picked, 'node', split_axis=0, concat_axis=0, tiled=True)  25.6 us
    dot_general x4, matrix products, one_layer(): jnp.einsum('tij,tjf->tif', adjacency, modulated, preferred_element_type=j...  24.4 us
    dot_general x4, local copies, waits for them, and re-layouts, one_layer(): jnp.einsum('tij,tjf->tif', adjacency, modulated, preferred_element_type=j...  21.9 us
    reshape x4, local copies, waits for them, and re-layouts, one_layer(): picked = picked.reshape(lead + (size_block * depth // lanes, lanes))  13.6 us
    convert_element_type x4, other arithmetic, one_layer(): (flat_products - high_part.astype(jnp.float32)).astype(jnp.bfloat16)  10.9 us
  transfers between devices with their start and end apart: 8, of which 8 were waited for; matrix products, arithmetic and copies ran while one was open for 22% of the time, Pallas kernels for 0%

profile of v3, /device:TPU:1, one launch (start us, length us, event | category | flops | bytes accessed | tf_op | source)
XLA Modules:
  0.0 309.2 jit_solution(9754163493258572953)
XLA Ops:
  11.8 10.5 %all-to-all-start = ((bf16[32,2,64,128]{3,2,1,0:T(8,128)(2,1)}), bf16[32,2,64,128]{3,2,1,0:T(8,128)(2,1)S(1)}, u32[]{:S(2)}, u32[]{:S(2)}) async-start(bf16[32,2,64,128]{3,2,1,0:T(8,128)(2,1)} %reshape.177), calls=%async_computation | async-start | bytes 2097152 | tf_op jit(solution)/shard_map/all_to_all | solution.py:49
  22.8 24.4 %all-to-all-done = bf16[32,2,64,128]{3,2,1,0:T(8,128)(2,1)S(1)} async-done(((bf16[32,2,64,128]{3,2,1,0:T(8,128)(2,1)}), bf16[32,2,64,128]{3,2,1,0:T(8,128)(2,1)S(1)}, u32[]{:S(2)}, u32[]{:S(2)}) %all-to-all-start) | async-done | bytes 1048608 | tf_op jit(solution)/shard_map/all_to_all | solution.py:49
  50.0 6.1 %convolution_bitcast_fusion.3 = f32[128,128,64]{1,2,0:T(8,128)} fusion(bf16[128,128,128]{2,1,0:T(8,128)(2,1)} %param.17, bf16[128,128,64]{1,2,0:T(8,128)(2,1)S(1)} %gather_fusion.1, f32[128,64]{1,0:T(8,128)S(1)} %copy.32, pred[128]{0:T(512)(128)(4,1)S(1)} %get-tuple-element.15), kind=kOutput, calls=%fused_computation.35 | convolution fusion | flops 272629760 | bytes 10518656 | tf_op jit(solution)/shard_map/tij,tjf->tif/dot_general | solution.py:53
  56.0 5.5 %copy.33 = f32[128,128,64]{0,2,1:T(8,128)} copy(f32[128,128,64]{1,2,0:T(8,128)} %convolution_bitcast_fusion.3) | data formatting | bytes 8388608 | tf_op jit(solution)/shard_map/tij,tjf->tif/dot_general | solution.py:53
  67.2 15.0 %all-to-all-start.1 = ((bf16[16,192,128]{2,1,0:T(8,128)(2,1)}), bf16[16,192,128]{2,1,0:T(8,128)(2,1)}, u32[]{:S(2)}, u32[]{:S(2)}) async-start(bf16[16,192,128]{2,1,0:T(8,128)(2,1)} %reshape.180), calls=%async_computation.1 | async-start | bytes 1572864 | tf_op jit(solution)/shard_map/all_to_all | solution.py:65
  84.8 20.4 %all-to-all-done.1 = bf16[16,192,128]{2,1,0:T(8,128)(2,1)} async-done(((bf16[16,192,128]{2,1,0:T(8,128)(2,1)}), bf16[16,192,128]{2,1,0:T(8,128)(2,1)}, u32[]{:S(2)}, u32[]{:S(2)}) %all-to-all-start.1) | async-done | bytes 786464 | tf_op jit(solution)/shard_map/all_to_all | solution.py:65
  113.7 4.0 %reshape.189 = bf16[32,2,64,128]{3,2,1,0:T(8,128)(2,1)} reshape(bf16[32,2,128,64]{3,2,1,0:T(8,128)(2,1)} %get-tuple-element.22) | data formatting | bytes 2097152 | tf_op jit(solution)/shard_map/reshape | solution.py:48
  117.7 4.8 %all-to-all-start.4 = ((bf16[32,2,64,128]{3,2,1,0:T(8,128)(2,1)}), bf16[32,2,64,128]{3,2,1,0:T(8,128)(2,1)S(1)}, u32[]{:S(2)}, u32[]{:S(2)}) async-start(bf16[32,2,64,128]{3,2,1,0:T(8,128)(2,1)} %reshape.189), calls=%async_computation.4 | async-start | bytes 2097152 | tf_op jit(solution)/shard_map/all_to_all | solution.py:49
  124.5 25.6 %all-to-all-done.4 = bf16[32,2,64,128]{3,2,1,0:T(8,128)(2,1)S(1)} async-done(((bf16[32,2,64,128]{3,2,1,0:T(8,128)(2,1)}), bf16[32,2,64,128]{3,2,1,0:T(8,128)(2,1)S(1)}, u32[]{:S(2)}, u32[]{:S(2)}) %all-to-all-start.4) | async-done | bytes 1048608 | tf_op jit(solution)/shard_map/all_to_all | solution.py:49
  150.1 5.1 %all-to-all-start.2 = ((bf16[32,2,64,128]{3,2,1,0:T(8,128)(2,1)}), bf16[32,2,64,128]{3,2,1,0:T(8,128)(2,1)}, u32[]{:S(2)}, u32[]{:S(2)}) async-start(bf16[32,2,64,128]{3,2,1,0:T(8,128)(2,1)} %reshape.183), calls=%async_computation.2 | async-start | bytes 2097152 | tf_op jit(solution)/shard_map/all_to_all | solution.py:49
  158.2 6.1 %convolution_bitcast_fusion.1 = f32[128,128,64]{1,2,0:T(8,128)} fusion(bf16[128,128,128]{2,1,0:T(8,128)(2,1)} %param.17, bf16[128,128,64]{1,2,0:T(8,128)(2,1)S(1)} %gather_fusion.5, f32[128,64]{1,0:T(8,128)S(1)} %copy.46, pred[128]{0:T(512)(128)(4,1)S(1)} %copy-done.11), kind=kOutput, calls=%fused_computation.33 | convolution fusion | flops 272629760 | bytes 10518656 | tf_op jit(solution)/shard_map/tij,tjf->tif/dot_general | solution.py:53
  164.3 5.5 %copy.47 = f32[128,128,64]{0,2,1:T(8,128)} copy(f32[128,128,64]{1,2,0:T(8,128)} %convolution_bitcast_fusion.1) | data formatting | bytes 8388608 | tf_op jit(solution)/shard_map/tij,tjf->tif/dot_general | solution.py:53
  175.4 5.6 %all-to-all-done.2 = bf16[32,2,64,128]{3,2,1,0:T(8,128)(2,1)} async-done(((bf16[32,2,64,128]{3,2,1,0:T(8,128)(2,1)}), bf16[32,2,64,128]{3,2,1,0:T(8,128)(2,1)}, u32[]{:S(2)}, u32[]{:S(2)}) %all-to-all-start.2) | async-done | bytes 1048608 | tf_op jit(solution)/shard_map/all_to_all | solution.py:49
  181.0 7.6 %all-to-all-start.5 = ((bf16[16,192,128]{2,1,0:T(8,128)(2,1)}), bf16[16,192,128]{2,1,0:T(8,128)(2,1)}, u32[]{:S(2)}, u32[]{:S(2)}) async-start(bf16[16,192,128]{2,1,0:T(8,128)(2,1)} %reshape.192), calls=%async_computation.5 | async-start | bytes 1572864 | tf_op jit(solution)/shard_map/all_to_all | solution.py:65
  193.3 6.2 %convolution_bitcast_fusion.2 = f32[128,128,64]{1,2,0:T(8,128)} fusion(bf16[128,128,128]{2,1,0:T(8,128)(2,1)} %param.17, bf16[128,128,64]{1,2,0:T(8,128)(2,1)S(1)} %gather_fusion.3, f32[128,64]{1,0:T(8,128)S(1)} %copy.32, pred[128]{0:T(512)(128)(4,1)S(1)} %copy-done.11), kind=kOutput, calls=%fused_computation.34 | convolution fusion | flops 272629760 | bytes 10518656 | tf_op jit(solution)/shard_map/tij,tjf->tif/dot_general | solution.py:53
  199.5 5.5 %copy.39 = f32[128,128,64]{0,2,1:T(8,128)} copy(f32[128,128,64]{1,2,0:T(8,128)} %convolution_bitcast_fusion.2) | data formatting | bytes 8388608 | tf_op jit(solution)/shard_map/tij,tjf->tif/dot_general | solution.py:53
  205.0 6.5 %all-to-all-done.5 = bf16[16,192,128]{2,1,0:T(8,128)(2,1)} async-done(((bf16[16,192,128]{2,1,0:T(8,128)(2,1)}), bf16[16,192,128]{2,1,0:T(8,128)(2,1)}, u32[]{:S(2)}, u32[]{:S(2)}) %all-to-all-start.5) | async-done | bytes 786464 | tf_op jit(solution)/shard_map/all_to_all | solution.py:65
  220.7 5.1 %all-to-all-start.6 = ((bf16[32,2,64,128]{3,2,1,0:T(8,128)(2,1)}), bf16[32,2,64,128]{3,2,1,0:T(8,128)(2,1)S(1)}, u32[]{:S(2)}, u32[]{:S(2)}) async-start(bf16[32,2,64,128]{3,2,1,0:T(8,128)(2,1)} %reshape.195), calls=%async_computation.6 | async-start | bytes 2097152 | tf_op jit(solution)/shard_map/all_to_all | solution.py:49
  231.4 21.7 %all-to-all-done.6 = bf16[32,2,64,128]{3,2,1,0:T(8,128)(2,1)S(1)} async-done(((bf16[32,2,64,128]{3,2,1,0:T(8,128)(2,1)}), bf16[32,2,64,128]{3,2,1,0:T(8,128)(2,1)S(1)}, u32[]{:S(2)}, u32[]{:S(2)}) %all-to-all-start.6) | async-done | bytes 1048608 | tf_op jit(solution)/shard_map/all_to_all | solution.py:49
  253.1 4.6 %all-to-all-start.3 = ((bf16[16,192,128]{2,1,0:T(8,128)(2,1)}), bf16[16,192,128]{2,1,0:T(8,128)(2,1)}, u32[]{:S(2)}, u32[]{:S(2)}) async-start(bf16[16,192,128]{2,1,0:T(8,128)(2,1)} %reshape.186), calls=%async_computation.3 | async-start | bytes 1572864 | tf_op jit(solution)/shard_map/all_to_all | solution.py:65
  260.6 6.1 %convolution_bitcast_fusion = f32[128,128,64]{1,2,0:T(8,128)} fusion(bf16[128,128,128]{2,1,0:T(8,128)(2,1)} %param.17, bf16[128,128,64]{1,2,0:T(8,128)(2,1)S(1)} %gather_fusion.7, f32[128,64]{1,0:T(8,128)S(1)} %copy.46, pred[128]{0:T(512)(128)(4,1)S(1)} %copy-done.11), kind=kOutput, calls=%fused_computation.32 | convolution fusion | flops 272629760 | bytes 10518656 | tf_op jit(solution)/shard_map/tij,tjf->tif/dot_general | solution.py:53
  266.7 5.5 %copy.53 = f32[128,128,64]{0,2,1:T(8,128)} copy(f32[128,128,64]{1,2,0:T(8,128)} %convolution_bitcast_fusion) | data formatting | bytes 8388608 | tf_op jit(solution)/shard_map/tij,tjf->tif/dot_general | solution.py:53
  280.6 4.5 %all-to-all-start.7 = ((bf16[16,192,128]{2,1,0:T(8,128)(2,1)}), bf16[16,192,128]{2,1,0:T(8,128)(2,1)S(1)}, u32[]{:S(2)}, u32[]{:S(2)}) async-start(bf16[16,192,128]{2,1,0:T(8,128)(2,1)} %reshape.198), calls=%async_computation.7 | async-start | bytes 1572864 | tf_op jit(solution)/shard_map/all_to_all | solution.py:65
  286.8 21.1 %all-to-all-done.7 = bf16[16,192,128]{2,1,0:T(8,128)(2,1)S(1)} async-done(((bf16[16,192,128]{2,1,0:T(8,128)(2,1)}), bf16[16,192,128]{2,1,0:T(8,128)(2,1)S(1)}, u32[]{:S(2)}, u32[]{:S(2)}) %all-to-all-start.7) | async-done | bytes 786464 | tf_op jit(solution)/shard_map/all_to_all | solution.py:65
  (137 shorter events, 75.7 us)
Async XLA Ops:
  0.0 22.3 %copy-start = (bf16[535,128]{1,0:T(8,128)(2,1)S(1)}, bf16[535,128]{1,0:T(8,128)(2,1)}, u32[]{:S(2)}) copy-start(bf16[535,128]{1,0:T(8,128)(2,1)} %param.25) | copy-start | bytes 410884
  7.9 14.4 %copy-start.21 = (s32[1,128]{1,0:T(1,128)S(1)}, s32[1,128]{1,0:T(1,128)}, u32[]{:S(2)}) copy-start(s32[1,128]{1,0:T(1,128)} %param.20) | copy-start | bytes 1540
  7.9 14.9 %copy-start.19 = (s32[1,128]{1,0:T(1,128)S(1)}, s32[1,128]{1,0:T(1,128)}, u32[]{:S(2)}) copy-start(s32[1,128]{1,0:T(1,128)} %param.19) | copy-start | bytes 1540
  7.9 14.9 %copy-start.20 = (s32[1,128]{1,0:T(1,128)S(1)}, s32[1,128]{1,0:T(1,128)}, u32[]{:S(2)}) copy-start(s32[1,128]{1,0:T(1,128)} %param.18) | copy-start | bytes 1540
  11.8 35.4 %all-to-all-start = ((bf16[32,2,64,128]{3,2,1,0:T(8,128)(2,1)}), bf16[32,2,64,128]{3,2,1,0:T(8,128)(2,1)S(1)}, u32[]{:S(2)}, u32[]{:S(2)}) async-start(bf16[32,2,64,128]{3,2,1,0:T(8,128)(2,1)} %reshape.177), calls=%async_computation | async-start | bytes 2097152 | tf_op jit(solution)/shard_map/all_to_all | solution.py:49
  22.8 27.2 %copy-start.10 = (pred[128]{0:T(512)(128)(4,1)}, pred[128]{0:T(512)(128)(4,1)S(1)}, u32[]{:S(2)}) copy-start(pred[128]{0:T(512)(128)(4,1)S(1)} %get-tuple-element.15) | copy-start | bytes 388
  22.8 26.2 %copy-start.12 = (s32[1024]{0:T(1024)}, s32[1024]{0:T(1024)S(1)}, u32[]{:S(2)}) copy-start(s32[1024]{0:T(1024)S(1)} %pad_clamp_fusion) | copy-start | bytes 12292
  61.5 2.7 copy-start.9
  67.2 37.9 %all-to-all-start.1 = ((bf16[16,192,128]{2,1,0:T(8,128)(2,1)}), bf16[16,192,128]{2,1,0:T(8,128)(2,1)}, u32[]{:S(2)}, u32[]{:S(2)}) async-start(bf16[16,192,128]{2,1,0:T(8,128)(2,1)} %reshape.180), calls=%async_computation.1 | async-start | bytes 1572864 | tf_op jit(solution)/shard_map/all_to_all | solution.py:65
  83.0 23.4 %copy-start.5 = (bf16[2,64,64]{2,1,0:T(8,128)(2,1)S(1)}, bf16[2,64,64]{2,1,0:T(8,128)(2,1)}, u32[]{:S(2)}) copy-start(bf16[2,64,64]{2,1,0:T(8,128)(2,1)} %param.26) | copy-start | bytes 49156
  83.1 23.7 %copy-start.4 = (bf16[384,64]{0,1:T(8,128)(2,1)S(1)}, bf16[384,64]{0,1:T(8,128)(2,1)}, u32[]{:S(2)}) copy-start(bf16[384,64]{0,1:T(8,128)(2,1)} %copy-done.3) | copy-start | bytes 147460
  84.8 22.1 %copy-start.14 = (f32[64]{0:T(128)}, f32[64]{0:T(128)S(1)}, u32[]{:S(2)}) copy-start(f32[64]{0:T(128)S(1)} %get-tuple-element.24) | copy-start | bytes 772
  113.7 8.9 %copy-start.2 = (bf16[32,2,128,64]{3,2,1,0:T(8,128)(2,1)S(1)}, bf16[32,2,128,64]{3,2,1,0:T(8,128)(2,1)}, u32[]{:S(2)}) copy-start(bf16[32,2,128,64]{3,2,1,0:T(8,128)(2,1)} %get-tuple-element.21) | copy-start | bytes 3145732
  117.7 32.4 %all-to-all-start.4 = ((bf16[32,2,64,128]{3,2,1,0:T(8,128)(2,1)}), bf16[32,2,64,128]{3,2,1,0:T(8,128)(2,1)S(1)}, u32[]{:S(2)}, u32[]{:S(2)}) async-start(bf16[32,2,64,128]{3,2,1,0:T(8,128)(2,1)} %reshape.189), calls=%async_computation.4 | async-start | bytes 2097152 | tf_op jit(solution)/shard_map/all_to_all | solution.py:49
  150.1 30.9 %all-to-all-start.2 = ((bf16[32,2,64,128]{3,2,1,0:T(8,128)(2,1)}), bf16[32,2,64,128]{3,2,1,0:T(8,128)(2,1)}, u32[]{:S(2)}, u32[]{:S(2)}) async-start(bf16[32,2,64,128]{3,2,1,0:T(8,128)(2,1)} %reshape.183), calls=%async_computation.2 | async-start | bytes 2097152 | tf_op jit(solution)/shard_map/all_to_all | solution.py:49
  181.0 30.5 %all-to-all-start.5 = ((bf16[16,192,128]{2,1,0:T(8,128)(2,1)}), bf16[16,192,128]{2,1,0:T(8,128)(2,1)}, u32[]{:S(2)}, u32[]{:S(2)}) async-start(bf16[16,192,128]{2,1,0:T(8,128)(2,1)} %reshape.192), calls=%async_computation.5 | async-start | bytes 1572864 | tf_op jit(solution)/shard_map/all_to_all | solution.py:65
  199.5 13.3 %copy-start.6 = (bf16[2,64,64]{2,1,0:T(8,128)(2,1)S(1)}, bf16[2,64,64]{2,1,0:T(8,128)(2,1)}, u32[]{:S(2)}) copy-start(bf16[2,64,64]{2,1,0:T(8,128)(2,1)} %param.26) | copy-start | bytes 49156
  199.5 13.6 %copy-start.15 = (f32[64]{0:T(128)S(1)}, f32[64]{0:T(128)}, u32[]{:S(2)}) copy-start(f32[64]{0:T(128)} %copy-done.14) | copy-start | bytes 772
  199.5 13.7 %copy-start.13 = (bf16[3]{0:T(256)(128)(2,1)S(1)}, bf16[3]{0:T(256)(128)(2,1)}, u32[]{:S(2)}) copy-start(bf16[3]{0:T(256)(128)(2,1)} %get-tuple-element.29) | copy-start | bytes 22
  220.7 32.5 %all-to-all-start.6 = ((bf16[32,2,64,128]{3,2,1,0:T(8,128)(2,1)}), bf16[32,2,64,128]{3,2,1,0:T(8,128)(2,1)S(1)}, u32[]{:S(2)}, u32[]{:S(2)}) async-start(bf16[32,2,64,128]{3,2,1,0:T(8,128)(2,1)} %reshape.195), calls=%async_computation.6 | async-start | bytes 2097152 | tf_op jit(solution)/shard_map/all_to_all | solution.py:49
  253.1 27.5 %all-to-all-start.3 = ((bf16[16,192,128]{2,1,0:T(8,128)(2,1)}), bf16[16,192,128]{2,1,0:T(8,128)(2,1)}, u32[]{:S(2)}, u32[]{:S(2)}) async-start(bf16[16,192,128]{2,1,0:T(8,128)(2,1)} %reshape.186), calls=%async_computation.3 | async-start | bytes 1572864 | tf_op jit(solution)/shard_map/all_to_all | solution.py:65
  277.9 30.4 %copy-start.16 = (f32[64]{0:T(128)S(1)}, f32[64]{0:T(128)}, u32[]{:S(2)}) copy-start(f32[64]{0:T(128)} %get-tuple-element.23) | copy-start | bytes 772
  280.6 27.2 %all-to-all-start.7 = ((bf16[16,192,128]{2,1,0:T(8,128)(2,1)}), bf16[16,192,128]{2,1,0:T(8,128)(2,1)S(1)}, u32[]{:S(2)}, u32[]{:S(2)}) async-start(bf16[16,192,128]{2,1,0:T(8,128)(2,1)} %reshape.198), calls=%async_computation.7 | async-start | bytes 1572864 | tf_op jit(solution)/shard_map/all_to_all | solution.py:65
  285.1 24.1 %copy-start.1 = (bf16[535,128]{1,0:T(8,128)(2,1)S(1)}, bf16[535,128]{1,0:T(8,128)(2,1)}, u32[]{:S(2)}) copy-start(bf16[535,128]{1,0:T(8,128)(2,1)} %param.25) | copy-start | bytes 410884
  (6 other events, 9.2 us)

commit v4 on v2

--- a/solution.py
+++ b/solution.py
@@ -48,12 +48,11 @@
         products = jnp.einsum(
             "tij,tjf->tif", adjacency, modulated, preferred_element_type=jnp.float32
         )
-        flat_products = products.reshape(tiles_here, -1)
-        high_part = flat_products.astype(jnp.bfloat16)
-        low_part = (flat_products - high_part.astype(jnp.float32)).astype(jnp.bfloat16)
-        partial_sum = jnp.dot(dst_onehot, high_part, preferred_element_type=jnp.float32) + jnp.dot(
-            dst_onehot, low_part, preferred_element_type=jnp.float32
-        )
+        high_part = products.astype(jnp.bfloat16)
+        low_part = (products - high_part.astype(jnp.float32)).astype(jnp.bfloat16)
+        partial_sum = jnp.einsum(
+            "mt,tif->mif", dst_onehot, high_part, preferred_element_type=jnp.float32
+        ) + jnp.einsum("mt,tif->mif", dst_onehot, low_part, preferred_element_type=jnp.float32)
         partial_sum = partial_sum.astype(jnp.bfloat16).reshape(
             lax.axis_size("tile"), own_blocks * size_block, width
         )

time: 283 us -> 284 us (level)
  other arithmetic: 15.5 us -> 7.47 us
  local copies, waits for them, and re-layouts: 31.9 us -> 39.7 us
    convert_element_type x0 -> x6, local copies, waits for them, and re-layouts: none -> 29.8 us  [the longest x2 13.5 us: body(): low_part = (products - high_part.astype(jnp.float32)).astype(jnp.bfloat16)]
    dot_general x2 -> x0, local copies, waits for them, and re-layouts: 18.7 us -> none  [body(): jnp.einsum('tij,tjf->tif', adjacency, modulated, preferred_element_type=j...]
    convert_element_type x2 -> x0, other arithmetic: 8.06 us -> none  [body(): (flat_products - high_part.astype(jnp.float32)).astype(jnp.bfloat16)]
    reshape x2 -> x0, local copies, waits for them, and re-layouts: 4.2 us -> none  [body(): partial_sum.astype(jnp.bfloat16)]
where the time goes in v4:
time: 284 us; the launch traced here: 283 us
  waiting for transfers between devices  125 us (44%)
  blocking collectives  55.9 us (20%)
  local copies, waits for them, and re-layouts  39.7 us (14%)
  starting transfers between devices  28.4 us (10%)
  matrix products  26.6 us (9%)
  other arithmetic  7.47 us (3%)
    all_to_all x2, waiting for transfers between devices, body(): lax.all_to_all(partial_sum, 'tile', split_axis=0, concat_axis=0, tiled=True)  76.4 us
    all_to_all x1, blocking collectives, body(): lax.all_to_all(picked, 'node', split_axis=0, concat_axis=0, tiled=True)  55.9 us
    all_to_all x1, waiting for transfers between devices, body(): lax.all_to_all(picked, 'node', split_axis=0, concat_axis=0, tiled=True)  48.6 us
    dot_general x2, matrix products, body(): jnp.einsum('tij,tjf->tif', adjacency, modulated, preferred_element_type=j...  18.5 us
    all_to_all x2, starting transfers between devices, body(): lax.all_to_all(partial_sum, 'tile', split_axis=0, concat_axis=0, tiled=True)  17.9 us
    convert_element_type x2, local copies, waits for them, and re-layouts, body(): low_part = (products - high_part.astype(jnp.float32)).astype(jnp.bfloat16)  13.5 us
    convert_element_type x2, local copies, waits for them, and re-layouts, body(): high_part = products.astype(jnp.bfloat16)  13.2 us
    all_to_all x1, starting transfers between devices, body(): lax.all_to_all(picked, 'node', split_axis=0, concat_axis=0, tiled=True)  10.5 us
  transfers between devices with their start and end apart: 3, of which 3 were waited for; matrix products, arithmetic and copies ran while one was open for 0% of the time, Pallas kernels for 0%

profile of v4, /device:TPU:1, one launch (start us, length us, event | category | flops | bytes accessed | tf_op | source)
XLA Modules:
  0.0 283.4 jit_solution(18382469544467683050)
XLA Ops:
  2.2 0.7 iota_compare_fusion.3
  3.1 1.0 broadcast_multiply_fusion.1
  4.1 0.9 gather_fusion
  5.1 1.7 select_select_fusion.1
  6.8 10.5 %all-to-all-start = ((bf16[32,2,128,128]{3,2,1,0:T(8,128)(2,1)}), bf16[32,2,128,128]{3,2,1,0:T(8,128)(2,1)S(1)}, u32[]{:S(2)}, u32[]{:S(2)}) async-start(bf16[32,2,128,128]{3,2,1,0:T(8,128)(2,1)} %select_select_fusion.1), calls=%async_computation | async-start | bytes 4194304 | tf_op jit(solution)/shard_map/all_to_all | solution.py:43
  17.6 48.6 %all-to-all-done = bf16[32,2,128,128]{3,2,1,0:T(8,128)(2,1)S(1)} async-done(((bf16[32,2,128,128]{3,2,1,0:T(8,128)(2,1)}), bf16[32,2,128,128]{3,2,1,0:T(8,128)(2,1)S(1)}, u32[]{:S(2)}, u32[]{:S(2)}) %all-to-all-start) | async-done | bytes 2097184 | tf_op jit(solution)/shard_map/all_to_all | solution.py:43
  66.2 3.1 %gather_fusion.1 = bf16[128,128,128]{2,1,0:T(8,128)(2,1)} fusion(bf16[64,128,128]{2,1,0:T(8,128)(2,1)S(1)} %bitcast.79, s32[1024]{0:T(1024)S(1)} %pad_clamp_fusion), kind=kCustom, calls=%fused_computation.1.clone | custom fusion | bytes 8389120 | tf_op jit(solution)/shard_map/jit(_take)/gather | solution.py:46
  69.2 9.2 %fusion.1 = (bf16[128,128,128]{1,2,0:T(8,128)(2,1)}, bf16[128,128,128]{1,2,0:T(8,128)(2,1)}) fusion(bf16[128,128,128]{2,1,0:T(8,128)(2,1)} %param.17, bf16[128,128,128]{2,1,0:T(8,128)(2,1)} %gather_fusion.1, f32[128,128]{1,0:T(8,128)S(1)} %fusion.12, pred[128]{0:T(512)(128)(4,1)S(1)} %get-tuple-element.11), kind=kOutput, calls=%fused_computation.9 | convolution fusion | flops 553648128 | bytes 16842880 | tf_op jit(solution)/shard_map/tij,tjf->tif/dot_general | solution.py:48
  78.5 6.8 %copy.29 = bf16[128,128,128]{2,0,1:T(8,128)(2,1)} copy(bf16[128,128,128]{1,2,0:T(8,128)(2,1)} %get-tuple-element.9) | data formatting | bytes 8388608 | tf_op jit(solution)/shard_map/convert_element_type | solution.py:52
  85.2 6.6 %copy.28 = bf16[128,128,128]{2,0,1:T(8,128)(2,1)} copy(bf16[128,128,128]{1,2,0:T(8,128)(2,1)} %get-tuple-element.10) | data formatting | bytes 8388608 | tf_op jit(solution)/shard_map/convert_element_type | solution.py:51
  91.9 3.0 %fusion.23 = f32[48,128,128]{2,0,1:T(8,128)S(1)} fusion(bf16[128,128,128]{2,0,1:T(8,128)(2,1)} %copy.28, s32[128]{0:T(128)S(1)} %bitcast.89), kind=kOutput, calls=%fused_computation.46 | convolution fusion | flops 201332736 | bytes 7340544 | tf_op jit(solution)/shard_map/mt,tif->mif/dot_general | solution.py:53
  96.1 1.6 copy.30
  97.6 12.4 %all-to-all-start.1 = ((bf16[16,384,128]{2,1,0:T(8,128)(2,1)}), bf16[16,384,128]{2,1,0:T(8,128)(2,1)S(1)}, u32[]{:S(2)}, u32[]{:S(2)}) async-start(bf16[16,384,128]{2,1,0:T(8,128)(2,1)} %bitcast.11), calls=%async_computation.1 | async-start | bytes 3145728 | tf_op jit(solution)/shard_map/all_to_all | solution.py:59
  110.6 38.0 %all-to-all-done.1 = bf16[16,384,128]{2,1,0:T(8,128)(2,1)S(1)} async-done(((bf16[16,384,128]{2,1,0:T(8,128)(2,1)}), bf16[16,384,128]{2,1,0:T(8,128)(2,1)S(1)}, u32[]{:S(2)}, u32[]{:S(2)}) %all-to-all-start.1) | async-done | bytes 1572896 | tf_op jit(solution)/shard_map/all_to_all | solution.py:59
  149.4 0.9 gather_fusion.2
  150.7 55.9 %all_to_all.20 = bf16[32,2,128,128]{3,2,1,0:T(8,128)(2,1)S(1)} all-to-all(bf16[32,2,128,128]{3,2,1,0:T(8,128)(2,1)S(1)} %select_select_fusion), channel_id=1, replica_groups=mesh['node'=32,'tile'=16] {'node'}, dimensions={0} | all-to-all | bytes 4194304 | tf_op jit(solution)/shard_map/all_to_all | solution.py:43
  206.6 3.1 %gather_fusion.3 = bf16[128,128,128]{2,1,0:T(8,128)(2,1)} fusion(bf16[64,128,128]{2,1,0:T(8,128)(2,1)S(1)} %bitcast.80, s32[1024]{0:T(1024)S(1)} %pad_clamp_fusion), kind=kCustom, calls=%fused_computation.3.clone | custom fusion | bytes 8389120 | tf_op jit(solution)/shard_map/jit(_take)/gather | solution.py:46
  209.7 9.2 %fusion = (bf16[128,128,128]{1,2,0:T(8,128)(2,1)}, bf16[128,128,128]{1,2,0:T(8,128)(2,1)}) fusion(bf16[128,128,128]{2,1,0:T(8,128)(2,1)} %param.17, bf16[128,128,128]{2,1,0:T(8,128)(2,1)} %gather_fusion.3, f32[128,128]{1,0:T(8,128)S(1)} %fusion.12, pred[128]{0:T(512)(128)(4,1)S(1)} %get-tuple-element.11), kind=kOutput, calls=%fused_computation.6 | convolution fusion | flops 553648128 | bytes 16842880 | tf_op jit(solution)/shard_map/tij,tjf->tif/dot_general | solution.py:48
  218.9 6.8 %copy.37 = bf16[128,128,128]{2,0,1:T(8,128)(2,1)} copy(bf16[128,128,128]{1,2,0:T(8,128)(2,1)} %get-tuple-element.6) | data formatting | bytes 8388608 | tf_op jit(solution)/shard_map/convert_element_type | solution.py:52
  225.7 6.6 %copy.36 = bf16[128,128,128]{2,0,1:T(8,128)(2,1)} copy(bf16[128,128,128]{1,2,0:T(8,128)(2,1)} %get-tuple-element.8) | data formatting | bytes 8388608 | tf_op jit(solution)/shard_map/convert_element_type | solution.py:51
  232.3 3.0 %fusion.20 = f32[48,128,128]{2,0,1:T(8,128)S(1)} fusion(bf16[128,128,128]{2,0,1:T(8,128)(2,1)} %copy.36, s32[128]{0:T(128)S(1)} %bitcast.91), kind=kOutput, calls=%fused_computation.45 | convolution fusion | flops 201332736 | bytes 7340544 | tf_op jit(solution)/shard_map/mt,tif->mif/dot_general | solution.py:53
  236.4 1.6 copy.38
  238.0 5.5 %all-to-all-start.3 = ((bf16[16,384,128]{2,1,0:T(8,128)(2,1)}), bf16[16,384,128]{2,1,0:T(8,128)(2,1)S(1)}, u32[]{:S(2)}, u32[]{:S(2)}) async-start(bf16[16,384,128]{2,1,0:T(8,128)(2,1)} %bitcast.23), calls=%async_computation.3 | async-start | bytes 3145728 | tf_op jit(solution)/shard_map/all_to_all | solution.py:59
  243.6 38.4 %all-to-all-done.3 = bf16[16,384,128]{2,1,0:T(8,128)(2,1)S(1)} async-done(((bf16[16,384,128]{2,1,0:T(8,128)(2,1)}), bf16[16,384,128]{2,1,0:T(8,128)(2,1)S(1)}, u32[]{:S(2)}, u32[]{:S(2)}) %all-to-all-start.3) | async-done | bytes 1572896 | tf_op jit(solution)/shard_map/all_to_all | solution.py:59
  (61 shorter events, 8.0 us)
Async XLA Ops:
  0.0 17.3 %copy-start = (bf16[535,128]{1,0:T(8,128)(2,1)S(1)}, bf16[535,128]{1,0:T(8,128)(2,1)}, u32[]{:S(2)}) copy-start(bf16[535,128]{1,0:T(8,128)(2,1)} %param.25) | copy-start | bytes 410884
  5.1 12.2 %copy-start.8 = (s32[1,128]{1,0:T(1,128)S(1)}, s32[1,128]{1,0:T(1,128)}, u32[]{:S(2)}) copy-start(s32[1,128]{1,0:T(1,128)} %param.19) | copy-start | bytes 1540
  5.1 12.2 %copy-start.9 = (s32[1,128]{1,0:T(1,128)S(1)}, s32[1,128]{1,0:T(1,128)}, u32[]{:S(2)}) copy-start(s32[1,128]{1,0:T(1,128)} %param.18) | copy-start | bytes 1540
  5.1 12.2 %copy-start.10 = (s32[1,128]{1,0:T(1,128)S(1)}, s32[1,128]{1,0:T(1,128)}, u32[]{:S(2)}) copy-start(s32[1,128]{1,0:T(1,128)} %param.20) | copy-start | bytes 1540
  6.8 59.4 %all-to-all-start = ((bf16[32,2,128,128]{3,2,1,0:T(8,128)(2,1)}), bf16[32,2,128,128]{3,2,1,0:T(8,128)(2,1)S(1)}, u32[]{:S(2)}, u32[]{:S(2)}) async-start(bf16[32,2,128,128]{3,2,1,0:T(8,128)(2,1)} %select_select_fusion.1), calls=%async_computation | async-start | bytes 4194304 | tf_op jit(solution)/shard_map/all_to_all | solution.py:43
  85.2 6.6 %copy-start.6 = (s32[1,128]{1,0:T(1,128)S(1)}, s32[1,128]{1,0:T(1,128)}, u32[]{:S(2)}) copy-start(s32[1,128]{1,0:T(1,128)} %param.21) | copy-start | bytes 1540
  91.9 3.4 %copy-start.2 = (bf16[128,128,128]{2,0,1:T(8,128)(2,1)S(1)}, bf16[128,128,128]{2,0,1:T(8,128)(2,1)}, u32[]{:S(2)}) copy-start(bf16[128,128,128]{2,0,1:T(8,128)(2,1)} %copy.29) | copy-start | bytes 12582916
  96.0 14.0 %copy-start.5 = (bf16[2,64,64]{2,1,0:T(8,128)(2,1)S(1)}, bf16[2,64,64]{2,1,0:T(8,128)(2,1)}, u32[]{:S(2)}) copy-start(bf16[2,64,64]{2,1,0:T(8,128)(2,1)} %param.26) | copy-start | bytes 49156
  96.0 14.5 %copy-start.7 = (f32[2,64]{1,0:T(2,128)S(1)}, f32[2,64]{1,0:T(2,128)}, u32[]{:S(2)}) copy-start(f32[2,64]{1,0:T(2,128)} %param.27) | copy-start | bytes 1540
  96.0 53.2 %copy-start.4 = (bf16[384,128]{1,0:T(8,128)(2,1)S(1)}, bf16[384,128]{1,0:T(8,128)(2,1)}, u32[]{:S(2)}) copy-start(bf16[384,128]{1,0:T(8,128)(2,1)} %param.16) | copy-start | bytes 294916
  97.6 51.0 %all-to-all-start.1 = ((bf16[16,384,128]{2,1,0:T(8,128)(2,1)}), bf16[16,384,128]{2,1,0:T(8,128)(2,1)S(1)}, u32[]{:S(2)}, u32[]{:S(2)}) async-start(bf16[16,384,128]{2,1,0:T(8,128)(2,1)} %bitcast.11), calls=%async_computation.1 | async-start | bytes 3145728 | tf_op jit(solution)/shard_map/all_to_all | solution.py:59
  232.3 3.4 %copy-start.3 = (bf16[128,128,128]{2,0,1:T(8,128)(2,1)S(1)}, bf16[128,128,128]{2,0,1:T(8,128)(2,1)}, u32[]{:S(2)}) copy-start(bf16[128,128,128]{2,0,1:T(8,128)(2,1)} %copy.37) | copy-start | bytes 12582916
  235.7 47.7 %copy-start.1 = (bf16[535,128]{1,0:T(8,128)(2,1)S(1)}, bf16[535,128]{1,0:T(8,128)(2,1)}, u32[]{:S(2)}) copy-start(bf16[535,128]{1,0:T(8,128)(2,1)} %param.25) | copy-start | bytes 410884
  238.0 44.0 %all-to-all-start.3 = ((bf16[16,384,128]{2,1,0:T(8,128)(2,1)}), bf16[16,384,128]{2,1,0:T(8,128)(2,1)S(1)}, u32[]{:S(2)}, u32[]{:S(2)}) async-start(bf16[16,384,128]{2,1,0:T(8,128)(2,1)} %bitcast.23), calls=%async_computation.3 | async-start | bytes 3145728 | tf_op jit(solution)/shard_map/all_to_all | solution.py:59

commit v5 on v2

--- a/solution.py
+++ b/solution.py
@@ -46,7 +46,7 @@
         source_rows = jnp.take(source, slot_index, axis=0)
         modulated = (source_rows * rel_rows[:, None, :]).astype(jnp.bfloat16)
         products = jnp.einsum(
-            "tij,tjf->tif", adjacency, modulated, preferred_element_type=jnp.float32
+            "tij,tjf->tfi", adjacency, modulated, preferred_element_type=jnp.float32
         )
         flat_products = products.reshape(tiles_here, -1)
         high_part = flat_products.astype(jnp.bfloat16)
@@ -55,10 +55,11 @@
             dst_onehot, low_part, preferred_element_type=jnp.float32
         )
         partial_sum = partial_sum.astype(jnp.bfloat16).reshape(
-            lax.axis_size("tile"), own_blocks * size_block, width
+            lax.axis_size("tile"), own_blocks, width, size_block
         )
         received = lax.all_to_all(partial_sum, "tile", split_axis=0, concat_axis=0, tiled=True)
         summed = jnp.sum(received.astype(jnp.float32), axis=0).astype(jnp.bfloat16)
+        summed = jnp.swapaxes(summed, 1, 2).reshape(own_blocks * size_block, width)
         mixer = jnp.kron(jnp.eye(query_count, dtype=jnp.bfloat16), mix_weight[layer])
         mixed = jnp.dot(summed, mixer, preferred_element_type=jnp.float32).reshape(
             -1, query_count, depth

time: 283 us -> 263 us (0.929)
  local copies, waits for them, and re-layouts: 31.9 us -> 12.3 us
  other arithmetic: 15.5 us -> 7.53 us
  matrix products: 25.3 us -> 32.9 us
    dot_general x2 -> x0, local copies, waits for them, and re-layouts: 18.7 us -> none  [body(): jnp.einsum('tij,tjf->tif', adjacency, modulated, preferred_element_type=j...]
    convert_element_type x2 -> x0, other arithmetic: 8.06 us -> none  [body(): (flat_products - high_part.astype(jnp.float32)).astype(jnp.bfloat16)]
    dot_general x2, matrix products: 3.09 us -> 10.4 us  [body(): jnp.dot(dst_onehot, low_part, preferred_element_type=jnp.float32)]
    dot_general x2, matrix products: 3.08 us -> 9.74 us  [body(): jnp.dot(dst_onehot, high_part, preferred_element_type=jnp.float32)]
    dot_general x2, matrix products: 18.4 us -> 12 us  [body(): jnp.einsum('tij,tjf->tfi', adjacency, modulated, preferred_element_type=j...]
    reshape x2 -> x0, local copies, waits for them, and re-layouts: 4.2 us -> none  [body(): partial_sum.astype(jnp.bfloat16)]
    unnamed x18, local copies, waits for them, and re-layouts: 0.05 us -> 3.2 us
where the time goes in v5:
time: 263 us; the launch traced here: 262 us
  waiting for transfers between devices  125 us (48%)
  blocking collectives  55.9 us (21%)
  matrix products  32.9 us (13%)
  starting transfers between devices  28.4 us (11%)
  local copies, waits for them, and re-layouts  12.3 us (5%)
  other arithmetic  7.53 us (3%)
    all_to_all x2, waiting for transfers between devices, body(): lax.all_to_all(partial_sum, 'tile', split_axis=0, concat_axis=0, tiled=True)  76.4 us
    all_to_all x1, blocking collectives, body(): lax.all_to_all(picked, 'node', split_axis=0, concat_axis=0, tiled=True)  55.9 us
    all_to_all x1, waiting for transfers between devices, body(): lax.all_to_all(picked, 'node', split_axis=0, concat_axis=0, tiled=True)  48.6 us
    all_to_all x2, starting transfers between devices, body(): lax.all_to_all(partial_sum, 'tile', split_axis=0, concat_axis=0, tiled=True)  17.9 us
    dot_general x2, matrix products, body(): jnp.einsum('tij,tjf->tfi', adjacency, modulated, preferred_element_type=j...  12 us
    all_to_all x1, starting transfers between devices, body(): lax.all_to_all(picked, 'node', split_axis=0, concat_axis=0, tiled=True)  10.5 us
    dot_general x2, matrix products, body(): jnp.dot(dst_onehot, low_part, preferred_element_type=jnp.float32)  10.4 us
    dot_general x2, matrix products, body(): jnp.dot(dst_onehot, high_part, preferred_element_type=jnp.float32)  9.74 us
  transfers between devices with their start and end apart: 3, of which 3 were waited for; matrix products, arithmetic and copies ran while one was open for 0% of the time, Pallas kernels for 0%

profile of v5, /device:TPU:1, one launch (start us, length us, event | category | flops | bytes accessed | tf_op | source)
XLA Modules:
  0.0 262.4 jit_solution(1402456178087979136)
XLA Ops:
  0.0 0.7 compare_and_fusion.1
  1.4 0.7 convert.6
  2.2 0.7 iota_compare_fusion.7
  3.1 1.0 broadcast_multiply_fusion.1
  4.1 0.9 gather_fusion
  5.1 1.7 select_select_fusion.1
  6.8 10.5 %all-to-all-start = ((bf16[32,2,128,128]{3,2,1,0:T(8,128)(2,1)}), bf16[32,2,128,128]{3,2,1,0:T(8,128)(2,1)S(1)}, u32[]{:S(2)}, u32[]{:S(2)}) async-start(bf16[32,2,128,128]{3,2,1,0:T(8,128)(2,1)} %select_select_fusion.1), calls=%async_computation | async-start | bytes 4194304 | tf_op jit(solution)/shard_map/all_to_all | solution.py:43
  17.6 48.6 %all-to-all-done = bf16[32,2,128,128]{3,2,1,0:T(8,128)(2,1)S(1)} async-done(((bf16[32,2,128,128]{3,2,1,0:T(8,128)(2,1)}), bf16[32,2,128,128]{3,2,1,0:T(8,128)(2,1)S(1)}, u32[]{:S(2)}, u32[]{:S(2)}) %all-to-all-start) | async-done | bytes 2097184 | tf_op jit(solution)/shard_map/all_to_all | solution.py:43
  66.2 3.0 %gather_fusion.1 = bf16[128,128,128]{2,1,0:T(8,128)(2,1)} fusion(bf16[64,128,128]{2,1,0:T(8,128)(2,1)S(1)} %bitcast.91, s32[1024]{0:T(1024)S(1)} %pad_clamp_fusion), kind=kCustom, calls=%fused_computation.1.clone | custom fusion | bytes 8389120 | tf_op jit(solution)/shard_map/jit(_take)/gather | solution.py:46
  69.2 6.0 %fusion.6 = f32[128,128,128]{2,1,0:T(8,128)S(1)} fusion(bf16[128,128,128]{2,1,0:T(8,128)(2,1)} %param.17, bf16[128,128,128]{2,1,0:T(8,128)(2,1)} %gather_fusion.1, f32[128,128]{1,0:T(8,128)S(1)} %fusion.24, pred[128]{0:T(512)(128)(4,1)S(1)} %get-tuple-element.6), kind=kOutput, calls=%fused_computation.18 | convolution fusion | flops 545259520 | bytes 16842880 | tf_op jit(solution)/shard_map/tij,tjf->tfi/dot_general | solution.py:48
  75.2 4.9 %fusion.4 = f32[48,16384]{1,0:T(8,128)S(1)} fusion(f32[16,8,128,128]{3,2,1,0:T(8,128)S(1)} %bitcast.89, s32[128]{0:T(128)S(1)} %bitcast.105), kind=kOutput, calls=%fused_computation.16 | convolution fusion | flops 201332736 | bytes 11534848 | tf_op jit(solution)/shard_map/dot_general | solution.py:54
  80.1 5.3 %fusion.21 = bf16[6,8,128,128]{3,1,2,0:T(8,128)(2,1)S(1)} fusion(f32[48,16384]{1,0:T(8,128)S(1)} %fusion.4, f32[16,8,128,128]{3,2,1,0:T(8,128)S(1)} %bitcast.90, s32[128]{0:T(128)S(1)} %bitcast.106), kind=kOutput, calls=%fused_computation.31 | convolution fusion | flops 211294208 | bytes 13107712 | tf_op jit(solution)/shard_map/dot_general | solution.py:54
  85.5 1.6 copy.56
  87.0 12.4 %all-to-all-start.1 = ((bf16[16,3,128,128]{3,2,1,0:T(8,128)(2,1)}), bf16[16,3,128,128]{3,2,1,0:T(8,128)(2,1)S(1)}, u32[]{:S(2)}, u32[]{:S(2)}) async-start(bf16[16,3,128,128]{3,2,1,0:T(8,128)(2,1)} %bitcast.37), calls=%async_computation.1 | async-start | bytes 3145728 | tf_op jit(solution)/shard_map/all_to_all | solution.py:60
  100.0 38.0 %all-to-all-done.1 = bf16[16,3,128,128]{3,2,1,0:T(8,128)(2,1)S(1)} async-done(((bf16[16,3,128,128]{3,2,1,0:T(8,128)(2,1)}), bf16[16,3,128,128]{3,2,1,0:T(8,128)(2,1)S(1)}, u32[]{:S(2)}, u32[]{:S(2)}) %all-to-all-start.1) | async-done | bytes 1572896 | tf_op jit(solution)/shard_map/all_to_all | solution.py:60
  139.0 0.9 gather_fusion.2
  140.3 55.9 %all_to_all.20 = bf16[32,2,128,128]{3,2,1,0:T(8,128)(2,1)S(1)} all-to-all(bf16[32,2,128,128]{3,2,1,0:T(8,128)(2,1)S(1)} %select_select_fusion), channel_id=1, replica_groups=mesh['node'=32,'tile'=16] {'node'}, dimensions={0} | all-to-all | bytes 4194304 | tf_op jit(solution)/shard_map/all_to_all | solution.py:43
  196.2 3.0 %gather_fusion.3 = bf16[128,128,128]{2,1,0:T(8,128)(2,1)} fusion(bf16[64,128,128]{2,1,0:T(8,128)(2,1)S(1)} %bitcast.92, s32[1024]{0:T(1024)S(1)} %pad_clamp_fusion), kind=kCustom, calls=%fused_computation.3.clone | custom fusion | bytes 8389120 | tf_op jit(solution)/shard_map/jit(_take)/gather | solution.py:46
  199.2 6.0 %fusion.7 = f32[128,128,128]{2,1,0:T(8,128)S(1)} fusion(bf16[128,128,128]{2,1,0:T(8,128)(2,1)} %param.17, bf16[128,128,128]{2,1,0:T(8,128)(2,1)} %gather_fusion.3, f32[128,128]{1,0:T(8,128)S(1)} %fusion.24, pred[128]{0:T(512)(128)(4,1)S(1)} %get-tuple-element.6), kind=kOutput, calls=%fused_computation.19 | convolution fusion | flops 545259520 | bytes 16842880 | tf_op jit(solution)/shard_map/tij,tjf->tfi/dot_general | solution.py:48
  205.3 4.9 %fusion.5 = f32[48,16384]{1,0:T(8,128)S(1)} fusion(f32[16,8,128,128]{3,2,1,0:T(8,128)S(1)} %bitcast.87, s32[128]{0:T(128)S(1)} %bitcast.107), kind=kOutput, calls=%fused_computation.17 | convolution fusion | flops 201332736 | bytes 11534848 | tf_op jit(solution)/shard_map/dot_general | solution.py:54
  210.1 5.1 %fusion.18 = bf16[6,8,128,128]{3,1,2,0:T(8,128)(2,1)S(1)} fusion(f32[48,16384]{1,0:T(8,128)S(1)} %fusion.5, f32[16,8,128,128]{3,2,1,0:T(8,128)S(1)} %bitcast.88, s32[128]{0:T(128)S(1)} %bitcast.108), kind=kOutput, calls=%fused_computation.30 | convolution fusion | flops 211294208 | bytes 13107712 | tf_op jit(solution)/shard_map/dot_general | solution.py:54
  215.3 1.6 copy.58
  216.9 5.5 %all-to-all-start.3 = ((bf16[16,3,128,128]{3,2,1,0:T(8,128)(2,1)}), bf16[16,3,128,128]{3,2,1,0:T(8,128)(2,1)S(1)}, u32[]{:S(2)}, u32[]{:S(2)}) async-start(bf16[16,3,128,128]{3,2,1,0:T(8,128)(2,1)} %bitcast.43), calls=%async_computation.3 | async-start | bytes 3145728 | tf_op jit(solution)/shard_map/all_to_all | solution.py:60
  222.5 38.4 %all-to-all-done.3 = bf16[16,3,128,128]{3,2,1,0:T(8,128)(2,1)S(1)} async-done(((bf16[16,3,128,128]{3,2,1,0:T(8,128)(2,1)}), bf16[16,3,128,128]{3,2,1,0:T(8,128)(2,1)S(1)}, u32[]{:S(2)}, u32[]{:S(2)}) %all-to-all-start.3) | async-done | bytes 1572896 | tf_op jit(solution)/shard_map/all_to_all | solution.py:60
  (53 shorter events, 4.7 us)
Async XLA Ops:
  0.0 17.3 %copy-start = (bf16[535,128]{1,0:T(8,128)(2,1)S(1)}, bf16[535,128]{1,0:T(8,128)(2,1)}, u32[]{:S(2)}) copy-start(bf16[535,128]{1,0:T(8,128)(2,1)} %param.25) | copy-start | bytes 410884
  5.1 12.2 %copy-start.5 = (s32[1,128]{1,0:T(1,128)S(1)}, s32[1,128]{1,0:T(1,128)}, u32[]{:S(2)}) copy-start(s32[1,128]{1,0:T(1,128)} %param.19) | copy-start | bytes 1540
  5.1 12.2 %copy-start.6 = (s32[1,128]{1,0:T(1,128)S(1)}, s32[1,128]{1,0:T(1,128)}, u32[]{:S(2)}) copy-start(s32[1,128]{1,0:T(1,128)} %param.18) | copy-start | bytes 1540
  5.1 12.2 %copy-start.7 = (s32[1,128]{1,0:T(1,128)S(1)}, s32[1,128]{1,0:T(1,128)}, u32[]{:S(2)}) copy-start(s32[1,128]{1,0:T(1,128)} %param.20) | copy-start | bytes 1540
  6.8 59.4 %all-to-all-start = ((bf16[32,2,128,128]{3,2,1,0:T(8,128)(2,1)}), bf16[32,2,128,128]{3,2,1,0:T(8,128)(2,1)S(1)}, u32[]{:S(2)}, u32[]{:S(2)}) async-start(bf16[32,2,128,128]{3,2,1,0:T(8,128)(2,1)} %select_select_fusion.1), calls=%async_computation | async-start | bytes 4194304 | tf_op jit(solution)/shard_map/all_to_all | solution.py:43
  69.2 6.0 %copy-start.3 = (s32[1,128]{1,0:T(1,128)S(1)}, s32[1,128]{1,0:T(1,128)}, u32[]{:S(2)}) copy-start(s32[1,128]{1,0:T(1,128)} %param.21) | copy-start | bytes 1540
  85.4 14.0 %copy-start.2 = (bf16[2,64,64]{2,1,0:T(8,128)(2,1)S(1)}, bf16[2,64,64]{2,1,0:T(8,128)(2,1)}, u32[]{:S(2)}) copy-start(bf16[2,64,64]{2,1,0:T(8,128)(2,1)} %param.26) | copy-start | bytes 49156
  85.4 14.5 %copy-start.4 = (f32[2,64]{1,0:T(2,128)S(1)}, f32[2,64]{1,0:T(2,128)}, u32[]{:S(2)}) copy-start(f32[2,64]{1,0:T(2,128)} %param.27) | copy-start | bytes 1540
  85.4 53.4 %copy-start.1 = (bf16[384,128]{1,0:T(8,128)(2,1)S(1)}, bf16[384,128]{1,0:T(8,128)(2,1)}, u32[]{:S(2)}) copy-start(bf16[384,128]{1,0:T(8,128)(2,1)} %param.16) | copy-start | bytes 294916
  87.0 51.0 %all-to-all-start.1 = ((bf16[16,3,128,128]{3,2,1,0:T(8,128)(2,1)}), bf16[16,3,128,128]{3,2,1,0:T(8,128)(2,1)S(1)}, u32[]{:S(2)}, u32[]{:S(2)}) async-start(bf16[16,3,128,128]{3,2,1,0:T(8,128)(2,1)} %bitcast.37), calls=%async_computation.1 | async-start | bytes 3145728 | tf_op jit(solution)/shard_map/all_to_all | solution.py:60
  216.9 44.0 %all-to-all-start.3 = ((bf16[16,3,128,128]{3,2,1,0:T(8,128)(2,1)}), bf16[16,3,128,128]{3,2,1,0:T(8,128)(2,1)S(1)}, u32[]{:S(2)}, u32[]{:S(2)}) async-start(bf16[16,3,128,128]{3,2,1,0:T(8,128)(2,1)} %bitcast.43), calls=%async_computation.3 | async-start | bytes 3145728 | tf_op jit(solution)/shard_map/all_to_all | solution.py:60

commit v6 on v5

--- a/solution.py
+++ b/solution.py
@@ -49,10 +49,8 @@
             "tij,tjf->tfi", adjacency, modulated, preferred_element_type=jnp.float32
         )
         flat_products = products.reshape(tiles_here, -1)
-        high_part = flat_products.astype(jnp.bfloat16)
-        low_part = (flat_products - high_part.astype(jnp.float32)).astype(jnp.bfloat16)
-        partial_sum = jnp.dot(dst_onehot, high_part, preferred_element_type=jnp.float32) + jnp.dot(
-            dst_onehot, low_part, preferred_element_type=jnp.float32
+        partial_sum = jnp.dot(
+            dst_onehot, flat_products.astype(jnp.bfloat16), preferred_element_type=jnp.float32
         )
         partial_sum = partial_sum.astype(jnp.bfloat16).reshape(
             lax.axis_size("tile"), own_blocks, width, size_block

time: 263 us -> 248 us (0.943)
  matrix products: 32.9 us -> 18.1 us
    dot_general x4 -> x2, matrix products: 20.2 us -> 5.44 us  [body(): jnp.dot(dst_onehot, flat_products.astype(jnp.bfloat16), preferred_element...]
where the time goes in v6:
time: 248 us
  waiting for transfers between devices  125 us (50%)
  blocking collectives  55.9 us (23%)
  starting transfers between devices  28.4 us (11%)
  matrix products  18.1 us (7%)
  local copies, waits for them, and re-layouts  12.3 us (5%)
  other arithmetic  7.53 us (3%)
    all_to_all x2, waiting for transfers between devices, body(): lax.all_to_all(partial_sum, 'tile', split_axis=0, concat_axis=0, tiled=True)  76.4 us
    all_to_all x1, blocking collectives, body(): lax.all_to_all(picked, 'node', split_axis=0, concat_axis=0, tiled=True)  55.9 us
    all_to_all x1, waiting for transfers between devices, body(): lax.all_to_all(picked, 'node', split_axis=0, concat_axis=0, tiled=True)  48.6 us
    all_to_all x2, starting transfers between devices, body(): lax.all_to_all(partial_sum, 'tile', split_axis=0, concat_axis=0, tiled=True)  17.9 us
    dot_general x2, matrix products, body(): jnp.einsum('tij,tjf->tfi', adjacency, modulated, preferred_element_type=j...  12 us
    all_to_all x1, starting transfers between devices, body(): lax.all_to_all(picked, 'node', split_axis=0, concat_axis=0, tiled=True)  10.5 us
    gather x2, local copies, waits for them, and re-layouts, body(): source_rows = jnp.take(source, slot_index, axis=0)  6.05 us
    dot_general x2, matrix products, body(): jnp.dot(dst_onehot, flat_products.astype(jnp.bfloat16), preferred_element...  5.44 us
  transfers between devices with their start and end apart: 3, of which 3 were waited for; matrix products, arithmetic and copies ran while one was open for 0% of the time, Pallas kernels for 0%

profile of v6, /device:TPU:1, one launch (start us, length us, event | category | flops | bytes accessed | tf_op | source)
XLA Modules:
  0.0 247.6 jit_solution(15333263432076158320)
XLA Ops:
  0.0 0.7 compare_and_fusion.1
  0.7 0.7 compare_select_fusion
  1.4 0.7 convert.6
  2.2 0.7 iota_compare_fusion.5
  3.1 1.0 broadcast_multiply_fusion.1
  4.1 0.9 gather_fusion
  5.1 1.7 select_select_fusion.1
  6.8 10.5 %all-to-all-start = ((bf16[32,2,128,128]{3,2,1,0:T(8,128)(2,1)}), bf16[32,2,128,128]{3,2,1,0:T(8,128)(2,1)S(1)}, u32[]{:S(2)}, u32[]{:S(2)}) async-start(bf16[32,2,128,128]{3,2,1,0:T(8,128)(2,1)} %select_select_fusion.1), calls=%async_computation | async-start | bytes 4194304 | tf_op jit(solution)/shard_map/all_to_all | solution.py:43
  17.6 48.6 %all-to-all-done = bf16[32,2,128,128]{3,2,1,0:T(8,128)(2,1)S(1)} async-done(((bf16[32,2,128,128]{3,2,1,0:T(8,128)(2,1)}), bf16[32,2,128,128]{3,2,1,0:T(8,128)(2,1)S(1)}, u32[]{:S(2)}, u32[]{:S(2)}) %all-to-all-start) | async-done | bytes 2097184 | tf_op jit(solution)/shard_map/all_to_all | solution.py:43
  66.2 3.0 %gather_fusion.1 = bf16[128,128,128]{2,1,0:T(8,128)(2,1)} fusion(bf16[64,128,128]{2,1,0:T(8,128)(2,1)S(1)} %bitcast.75, s32[1024]{0:T(1024)S(1)} %pad_clamp_fusion), kind=kCustom, calls=%fused_computation.1.clone | custom fusion | bytes 8389120 | tf_op jit(solution)/shard_map/jit(_take)/gather | solution.py:46
  69.2 6.0 %fusion.13 = bf16[128,128,128]{2,1,0:T(8,128)(2,1)S(1)} fusion(bf16[128,128,128]{2,1,0:T(8,128)(2,1)} %param.17, bf16[128,128,128]{2,1,0:T(8,128)(2,1)} %gather_fusion.1, f32[128,128]{1,0:T(8,128)S(1)} %fusion.22, pred[128]{0:T(512)(128)(4,1)S(1)} %get-tuple-element.6), kind=kOutput, calls=%fused_computation.21 | convolution fusion | flops 547356672 | bytes 12648576 | tf_op jit(solution)/shard_map/tij,tjf->tfi/dot_general | solution.py:48
  75.2 2.7 %fusion.16 = bf16[6,8,128,128]{3,1,2,0:T(8,128)(2,1)S(1)} fusion(bf16[16,8,128,128]{3,2,1,0:T(8,128)(2,1)S(1)} %bitcast.80, s32[128]{0:T(128)S(1)} %bitcast.91), kind=kOutput, calls=%fused_computation.26 | convolution fusion | flops 202119168 | bytes 5767680 | tf_op jit(solution)/shard_map/dot_general | solution.py:52
  78.0 1.6 copy.56
  79.5 12.4 %all-to-all-start.1 = ((bf16[16,3,128,128]{3,2,1,0:T(8,128)(2,1)}), bf16[16,3,128,128]{3,2,1,0:T(8,128)(2,1)S(1)}, u32[]{:S(2)}, u32[]{:S(2)}) async-start(bf16[16,3,128,128]{3,2,1,0:T(8,128)(2,1)} %bitcast.37), calls=%async_computation.1 | async-start | bytes 3145728 | tf_op jit(solution)/shard_map/all_to_all | solution.py:58
  92.5 38.0 %all-to-all-done.1 = bf16[16,3,128,128]{3,2,1,0:T(8,128)(2,1)S(1)} async-done(((bf16[16,3,128,128]{3,2,1,0:T(8,128)(2,1)}), bf16[16,3,128,128]{3,2,1,0:T(8,128)(2,1)S(1)}, u32[]{:S(2)}, u32[]{:S(2)}) %all-to-all-start.1) | async-done | bytes 1572896 | tf_op jit(solution)/shard_map/all_to_all | solution.py:58
  131.5 0.9 gather_fusion.2
  132.8 55.9 %all_to_all.20 = bf16[32,2,128,128]{3,2,1,0:T(8,128)(2,1)S(1)} all-to-all(bf16[32,2,128,128]{3,2,1,0:T(8,128)(2,1)S(1)} %select_select_fusion), channel_id=1, replica_groups=mesh['node'=32,'tile'=16] {'node'}, dimensions={0} | all-to-all | bytes 4194304 | tf_op jit(solution)/shard_map/all_to_all | solution.py:43
  188.7 3.0 %gather_fusion.3 = bf16[128,128,128]{2,1,0:T(8,128)(2,1)} fusion(bf16[64,128,128]{2,1,0:T(8,128)(2,1)S(1)} %bitcast.76, s32[1024]{0:T(1024)S(1)} %pad_clamp_fusion), kind=kCustom, calls=%fused_computation.3.clone | custom fusion | bytes 8389120 | tf_op jit(solution)/shard_map/jit(_take)/gather | solution.py:46
  191.7 6.0 %fusion.12 = bf16[128,128,128]{2,1,0:T(8,128)(2,1)S(1)} fusion(bf16[128,128,128]{2,1,0:T(8,128)(2,1)} %param.17, bf16[128,128,128]{2,1,0:T(8,128)(2,1)} %gather_fusion.3, f32[128,128]{1,0:T(8,128)S(1)} %fusion.22, pred[128]{0:T(512)(128)(4,1)S(1)} %get-tuple-element.6), kind=kOutput, calls=%fused_computation.20 | convolution fusion | flops 547356672 | bytes 12648576 | tf_op jit(solution)/shard_map/tij,tjf->tfi/dot_general | solution.py:48
  197.7 2.7 %fusion.19 = bf16[6,8,128,128]{3,1,2,0:T(8,128)(2,1)S(1)} fusion(bf16[16,8,128,128]{3,2,1,0:T(8,128)(2,1)S(1)} %bitcast.79, s32[128]{0:T(128)S(1)} %bitcast.92), kind=kOutput, calls=%fused_computation.27 | convolution fusion | flops 202119168 | bytes 5767680 | tf_op jit(solution)/shard_map/dot_general | solution.py:52
  200.5 1.6 copy.58
  202.0 5.5 %all-to-all-start.3 = ((bf16[16,3,128,128]{3,2,1,0:T(8,128)(2,1)}), bf16[16,3,128,128]{3,2,1,0:T(8,128)(2,1)S(1)}, u32[]{:S(2)}, u32[]{:S(2)}) async-start(bf16[16,3,128,128]{3,2,1,0:T(8,128)(2,1)} %bitcast.43), calls=%async_computation.3 | async-start | bytes 3145728 | tf_op jit(solution)/shard_map/all_to_all | solution.py:58
  207.6 38.4 %all-to-all-done.3 = bf16[16,3,128,128]{3,2,1,0:T(8,128)(2,1)S(1)} async-done(((bf16[16,3,128,128]{3,2,1,0:T(8,128)(2,1)}), bf16[16,3,128,128]{3,2,1,0:T(8,128)(2,1)S(1)}, u32[]{:S(2)}, u32[]{:S(2)}) %all-to-all-start.3) | async-done | bytes 1572896 | tf_op jit(solution)/shard_map/all_to_all | solution.py:58
  246.9 0.7 add_convert_fusion
  (51 shorter events, 3.3 us)
Async XLA Ops:
  0.0 17.3 %copy-start = (bf16[535,128]{1,0:T(8,128)(2,1)S(1)}, bf16[535,128]{1,0:T(8,128)(2,1)}, u32[]{:S(2)}) copy-start(bf16[535,128]{1,0:T(8,128)(2,1)} %param.25) | copy-start | bytes 410884
  5.1 12.2 %copy-start.5 = (s32[1,128]{1,0:T(1,128)S(1)}, s32[1,128]{1,0:T(1,128)}, u32[]{:S(2)}) copy-start(s32[1,128]{1,0:T(1,128)} %param.19) | copy-start | bytes 1540
  5.1 12.2 %copy-start.6 = (s32[1,128]{1,0:T(1,128)S(1)}, s32[1,128]{1,0:T(1,128)}, u32[]{:S(2)}) copy-start(s32[1,128]{1,0:T(1,128)} %param.18) | copy-start | bytes 1540
  5.1 12.2 %copy-start.7 = (s32[1,128]{1,0:T(1,128)S(1)}, s32[1,128]{1,0:T(1,128)}, u32[]{:S(2)}) copy-start(s32[1,128]{1,0:T(1,128)} %param.20) | copy-start | bytes 1540
  6.8 59.4 %all-to-all-start = ((bf16[32,2,128,128]{3,2,1,0:T(8,128)(2,1)}), bf16[32,2,128,128]{3,2,1,0:T(8,128)(2,1)S(1)}, u32[]{:S(2)}, u32[]{:S(2)}) async-start(bf16[32,2,128,128]{3,2,1,0:T(8,128)(2,1)} %select_select_fusion.1), calls=%async_computation | async-start | bytes 4194304 | tf_op jit(solution)/shard_map/all_to_all | solution.py:43
  69.2 6.0 %copy-start.3 = (s32[1,128]{1,0:T(1,128)S(1)}, s32[1,128]{1,0:T(1,128)}, u32[]{:S(2)}) copy-start(s32[1,128]{1,0:T(1,128)} %param.21) | copy-start | bytes 1540
  77.9 14.0 %copy-start.2 = (bf16[2,64,64]{2,1,0:T(8,128)(2,1)S(1)}, bf16[2,64,64]{2,1,0:T(8,128)(2,1)}, u32[]{:S(2)}) copy-start(bf16[2,64,64]{2,1,0:T(8,128)(2,1)} %param.26) | copy-start | bytes 49156
  77.9 14.5 %copy-start.4 = (f32[2,64]{1,0:T(2,128)S(1)}, f32[2,64]{1,0:T(2,128)}, u32[]{:S(2)}) copy-start(f32[2,64]{1,0:T(2,128)} %param.27) | copy-start | bytes 1540
  77.9 53.4 %copy-start.1 = (bf16[384,128]{1,0:T(8,128)(2,1)S(1)}, bf16[384,128]{1,0:T(8,128)(2,1)}, u32[]{:S(2)}) copy-start(bf16[384,128]{1,0:T(8,128)(2,1)} %param.16) | copy-start | bytes 294916
  79.5 51.0 %all-to-all-start.1 = ((bf16[16,3,128,128]{3,2,1,0:T(8,128)(2,1)}), bf16[16,3,128,128]{3,2,1,0:T(8,128)(2,1)S(1)}, u32[]{:S(2)}, u32[]{:S(2)}) async-start(bf16[16,3,128,128]{3,2,1,0:T(8,128)(2,1)} %bitcast.37), calls=%async_computation.1 | async-start | bytes 3145728 | tf_op jit(solution)/shard_map/all_to_all | solution.py:58
  202.0 44.0 %all-to-all-start.3 = ((bf16[16,3,128,128]{3,2,1,0:T(8,128)(2,1)}), bf16[16,3,128,128]{3,2,1,0:T(8,128)(2,1)S(1)}, u32[]{:S(2)}, u32[]{:S(2)}) async-start(bf16[16,3,128,128]{3,2,1,0:T(8,128)(2,1)} %bitcast.43), calls=%async_computation.3 | async-start | bytes 3145728 | tf_op jit(solution)/shard_map/all_to_all | solution.py:58

commit v7 on v6

--- a/solution.py
+++ b/solution.py
@@ -55,8 +55,17 @@
         partial_sum = partial_sum.astype(jnp.bfloat16).reshape(
             lax.axis_size("tile"), own_blocks, width, size_block
         )
-        received = lax.all_to_all(partial_sum, "tile", split_axis=0, concat_axis=0, tiled=True)
-        summed = jnp.sum(received.astype(jnp.float32), axis=0).astype(jnp.bfloat16)
+        received = lax.all_to_all(
+            partial_sum[:, : own_blocks - 1], "tile", split_axis=0, concat_axis=0, tiled=True
+        )
+        summed_head = jnp.sum(received.astype(jnp.float32), axis=0).astype(jnp.bfloat16)
+        summed_tail = lax.psum_scatter(
+            partial_sum[:, own_blocks - 1].reshape(-1, size_block),
+            "tile",
+            scatter_dimension=0,
+            tiled=True,
+        )
+        summed = jnp.concatenate([summed_head, summed_tail[None]], axis=0)
         summed = jnp.swapaxes(summed, 1, 2).reshape(own_blocks * size_block, width)
         mixer = jnp.kron(jnp.eye(query_count, dtype=jnp.bfloat16), mix_weight[layer])
         mixed = jnp.dot(summed, mixer, preferred_element_type=jnp.float32).reshape(

time: 248 us -> 313 us (1.26)
  waiting for transfers between devices: 125 us -> 167 us
  between operations: 0.33 us -> 13.8 us
  starting transfers between devices: 28.4 us -> 37.8 us
  blocking collectives: 55.9 us -> 51.9 us
    reduce_scatter x0 -> x2, waiting for transfers between devices: none -> 63.5 us  [body(): lax.psum_scatter(partial_sum[:, own_blocks - 1].reshape(-1, size_block),...]
    all_to_all x2, waiting for transfers between devices: 76.4 us -> 54.4 us  [body(): lax.all_to_all(partial_sum[:, :own_blocks - 1], 'tile', split_axis=0, con...]
    all_to_all x2, starting transfers between devices: 17.9 us -> 27.2 us  [body(): lax.all_to_all(partial_sum[:, :own_blocks - 1], 'tile', split_axis=0, con...]
    all_to_all x1, blocking collectives: 55.9 us -> 51.9 us  [body(): lax.all_to_all(picked, 'node', split_axis=0, concat_axis=0, tiled=True)]
    slice x0 -> x4, local copies, waits for them, and re-layouts: none -> 3.77 us  [the longest x2 2.08 us: body(): partial_sum[:, :own_blocks - 1]]
  transfers between devices with their start and end apart: 3 -> 5, of which waited for: 3 -> 5; matrix products, arithmetic and copies ran while one was open for 0% -> 1% of each run, Pallas kernels for 0% -> 0%
where the time goes in v7:
time: 313 us; the launch traced here: 311 us
  waiting for transfers between devices  167 us (53%)
  blocking collectives  51.9 us (17%)
  starting transfers between devices  37.8 us (12%)
  matrix products  18.1 us (6%)
  between operations  13.8 us (4%)
  local copies, waits for them, and re-layouts  13.7 us (4%)
  other arithmetic  8.85 us (3%)
    reduce_scatter x2, waiting for transfers between devices, body(): lax.psum_scatter(partial_sum[:, own_blocks - 1].reshape(-1, size_block),...  63.5 us
    all_to_all x2, waiting for transfers between devices, body(): lax.all_to_all(partial_sum[:, :own_blocks - 1], 'tile', split_axis=0, con...  54.4 us
    all_to_all x1, blocking collectives, body(): lax.all_to_all(picked, 'node', split_axis=0, concat_axis=0, tiled=True)  51.9 us
    all_to_all x1, waiting for transfers between devices, body(): lax.all_to_all(picked, 'node', split_axis=0, concat_axis=0, tiled=True)  48.6 us
    all_to_all x2, starting transfers between devices, body(): lax.all_to_all(partial_sum[:, :own_blocks - 1], 'tile', split_axis=0, con...  27.2 us
    dot_general x2, matrix products, body(): jnp.einsum('tij,tjf->tfi', adjacency, modulated, preferred_element_type=j...  12 us
    all_to_all x1, starting transfers between devices, body(): lax.all_to_all(picked, 'node', split_axis=0, concat_axis=0, tiled=True)  10.5 us
  transfers between devices with their start and end apart: 5, of which 5 were waited for; matrix products, arithmetic and copies ran while one was open for 1% of the time, Pallas kernels for 0%

profile of v7, /device:TPU:1, one launch (start us, length us, event | category | flops | bytes accessed | tf_op | source)
XLA Modules:
  0.0 310.6 jit_solution(12147063517703566876)
XLA Ops:
  9.7 1.0 broadcast_multiply_fusion.1
  10.6 0.9 gather_fusion
  11.6 1.7 select_select_fusion.1
  13.3 10.5 %all-to-all-start = ((bf16[32,2,128,128]{3,2,1,0:T(8,128)(2,1)}), bf16[32,2,128,128]{3,2,1,0:T(8,128)(2,1)S(1)}, u32[]{:S(2)}, u32[]{:S(2)}) async-start(bf16[32,2,128,128]{3,2,1,0:T(8,128)(2,1)} %select_select_fusion.1), calls=%async_computation | async-start | bytes 4194304 | tf_op jit(solution)/shard_map/all_to_all | solution.py:43
  24.1 48.6 %all-to-all-done = bf16[32,2,128,128]{3,2,1,0:T(8,128)(2,1)S(1)} async-done(((bf16[32,2,128,128]{3,2,1,0:T(8,128)(2,1)}), bf16[32,2,128,128]{3,2,1,0:T(8,128)(2,1)S(1)}, u32[]{:S(2)}, u32[]{:S(2)}) %all-to-all-start) | async-done | bytes 2097184 | tf_op jit(solution)/shard_map/all_to_all | solution.py:43
  72.7 3.0 gather_fusion.1
  75.7 6.0 %fusion.13 = bf16[128,128,128]{2,1,0:T(8,128)(2,1)S(1)} fusion(bf16[128,128,128]{2,1,0:T(8,128)(2,1)} %param.17, bf16[128,128,128]{2,1,0:T(8,128)(2,1)} %gather_fusion.1, f32[128,128]{1,0:T(8,128)S(1)} %fusion.22, pred[128]{0:T(512)(128)(4,1)S(1)} %get-tuple-element.6), kind=kOutput, calls=%fused_computation.21 | convolution fusion | flops 547356672 | bytes 12648576 | tf_op jit(solution)/shard_map/tij,tjf->tfi/dot_general | solution.py:48
  81.7 2.7 fusion.16
  84.9 1.0 slice.50
  85.9 12.4 %all-to-all-start.1 = ((bf16[16,2,128,128]{3,2,1,0:T(8,128)(2,1)}), bf16[16,2,128,128]{3,2,1,0:T(8,128)(2,1)S(1)}, u32[]{:S(2)}, u32[]{:S(2)}) async-start(bf16[16,2,128,128]{3,2,1,0:T(8,128)(2,1)} %slice.50), calls=%async_computation.1 | async-start | bytes 2097152 | tf_op jit(solution)/shard_map/all_to_all | solution.py:58
  98.4 0.8 slice.51
  99.8 26.9 %all-to-all-done.1 = bf16[16,2,128,128]{3,2,1,0:T(8,128)(2,1)S(1)} async-done(((bf16[16,2,128,128]{3,2,1,0:T(8,128)(2,1)}), bf16[16,2,128,128]{3,2,1,0:T(8,128)(2,1)S(1)}, u32[]{:S(2)}, u32[]{:S(2)}) %all-to-all-start.1) | async-done | bytes 1048608 | tf_op jit(solution)/shard_map/all_to_all | solution.py:58
  126.9 31.9 %reduce-scatter.7.cloned.1.call-done = bf16[128,128]{1,0:T(8,128)(2,1)} async-done(((bf16[2048,128]{1,0:T(8,128)(2,1)}), bf16[128,128]{1,0:T(8,128)(2,1)}) %reduce-scatter.7.cloned.1.call-update) | async-done | bytes 32784 | tf_op jit(solution)/shard_map/reduce_scatter | solution.py:62
  158.8 0.8 maximum_bitcast_fusion
  160.3 0.9 gather_fusion.2
  161.6 51.9 %all_to_all.20 = bf16[32,2,128,128]{3,2,1,0:T(8,128)(2,1)S(1)} all-to-all(bf16[32,2,128,128]{3,2,1,0:T(8,128)(2,1)S(1)} %select_select_fusion), channel_id=1, replica_groups=mesh['node'=32,'tile'=16] {'node'}, dimensions={0} | all-to-all | bytes 4194304 | tf_op jit(solution)/shard_map/all_to_all | solution.py:43
  213.4 3.0 gather_fusion.3
  216.5 6.0 %fusion.12 = bf16[128,128,128]{2,1,0:T(8,128)(2,1)S(1)} fusion(bf16[128,128,128]{2,1,0:T(8,128)(2,1)} %param.17, bf16[128,128,128]{2,1,0:T(8,128)(2,1)} %gather_fusion.3, f32[128,128]{1,0:T(8,128)S(1)} %fusion.22, pred[128]{0:T(512)(128)(4,1)S(1)} %get-tuple-element.6), kind=kOutput, calls=%fused_computation.20 | convolution fusion | flops 547356672 | bytes 12648576 | tf_op jit(solution)/shard_map/tij,tjf->tfi/dot_general | solution.py:48
  222.4 2.7 fusion.19
  225.6 1.0 slice.52
  226.6 14.8 %all-to-all-start.3 = ((bf16[16,2,128,128]{3,2,1,0:T(8,128)(2,1)}), bf16[16,2,128,128]{3,2,1,0:T(8,128)(2,1)S(1)}, u32[]{:S(2)}, u32[]{:S(2)}) async-start(bf16[16,2,128,128]{3,2,1,0:T(8,128)(2,1)} %slice.52), calls=%async_computation.3 | async-start | bytes 2097152 | tf_op jit(solution)/shard_map/all_to_all | solution.py:58
  241.4 0.8 slice.53
  242.4 27.4 %all-to-all-done.3 = bf16[16,2,128,128]{3,2,1,0:T(8,128)(2,1)S(1)} async-done(((bf16[16,2,128,128]{3,2,1,0:T(8,128)(2,1)}), bf16[16,2,128,128]{3,2,1,0:T(8,128)(2,1)S(1)}, u32[]{:S(2)}, u32[]{:S(2)}) %all-to-all-start.3) | async-done | bytes 1048608 | tf_op jit(solution)/shard_map/all_to_all | solution.py:58
  270.0 31.7 %reduce-scatter.9.cloned.1.call-done = bf16[128,128]{1,0:T(8,128)(2,1)} async-done(((bf16[2048,128]{1,0:T(8,128)(2,1)}), bf16[128,128]{1,0:T(8,128)(2,1)}) %reduce-scatter.9.cloned.1.call-update) | async-done | bytes 32784 | tf_op jit(solution)/shard_map/reduce_scatter | solution.py:62
  (63 shorter events, 8.2 us)
Async XLA Ops:
  6.5 17.3 %copy-start = (bf16[535,128]{1,0:T(8,128)(2,1)S(1)}, bf16[535,128]{1,0:T(8,128)(2,1)}, u32[]{:S(2)}) copy-start(bf16[535,128]{1,0:T(8,128)(2,1)} %param.25) | copy-start | bytes 410884
  11.6 12.2 %copy-start.5 = (s32[1,128]{1,0:T(1,128)S(1)}, s32[1,128]{1,0:T(1,128)}, u32[]{:S(2)}) copy-start(s32[1,128]{1,0:T(1,128)} %param.19) | copy-start | bytes 1540
  11.6 12.2 %copy-start.6 = (s32[1,128]{1,0:T(1,128)S(1)}, s32[1,128]{1,0:T(1,128)}, u32[]{:S(2)}) copy-start(s32[1,128]{1,0:T(1,128)} %param.18) | copy-start | bytes 1540
  11.6 12.2 %copy-start.7 = (s32[1,128]{1,0:T(1,128)S(1)}, s32[1,128]{1,0:T(1,128)}, u32[]{:S(2)}) copy-start(s32[1,128]{1,0:T(1,128)} %param.20) | copy-start | bytes 1540
  13.3 59.4 %all-to-all-start = ((bf16[32,2,128,128]{3,2,1,0:T(8,128)(2,1)}), bf16[32,2,128,128]{3,2,1,0:T(8,128)(2,1)S(1)}, u32[]{:S(2)}, u32[]{:S(2)}) async-start(bf16[32,2,128,128]{3,2,1,0:T(8,128)(2,1)} %select_select_fusion.1), calls=%async_computation | async-start | bytes 4194304 | tf_op jit(solution)/shard_map/all_to_all | solution.py:43
  75.7 6.0 %copy-start.3 = (s32[1,128]{1,0:T(1,128)S(1)}, s32[1,128]{1,0:T(1,128)}, u32[]{:S(2)}) copy-start(s32[1,128]{1,0:T(1,128)} %param.21) | copy-start | bytes 1540
  84.5 14.8 %copy-start.2 = (bf16[2,64,64]{2,1,0:T(8,128)(2,1)S(1)}, bf16[2,64,64]{2,1,0:T(8,128)(2,1)}, u32[]{:S(2)}) copy-start(bf16[2,64,64]{2,1,0:T(8,128)(2,1)} %param.26) | copy-start | bytes 49156
  84.5 15.3 %copy-start.4 = (f32[2,64]{1,0:T(2,128)S(1)}, f32[2,64]{1,0:T(2,128)}, u32[]{:S(2)}) copy-start(f32[2,64]{1,0:T(2,128)} %param.27) | copy-start | bytes 1540
  84.9 75.3 %copy-start.1 = (bf16[384,128]{1,0:T(8,128)(2,1)S(1)}, bf16[384,128]{1,0:T(8,128)(2,1)}, u32[]{:S(2)}) copy-start(bf16[384,128]{1,0:T(8,128)(2,1)} %param.16) | copy-start | bytes 294916
  85.9 40.8 %all-to-all-start.1 = ((bf16[16,2,128,128]{3,2,1,0:T(8,128)(2,1)}), bf16[16,2,128,128]{3,2,1,0:T(8,128)(2,1)S(1)}, u32[]{:S(2)}, u32[]{:S(2)}) async-start(bf16[16,2,128,128]{3,2,1,0:T(8,128)(2,1)} %slice.50), calls=%async_computation.1 | async-start | bytes 2097152 | tf_op jit(solution)/shard_map/all_to_all | solution.py:58
  98.4 60.4 %reduce-scatter.7.cloned.1.call-start = ((), (), s32[]{:S(2)}) async-start(), calls=%async_computation.6 | async-start | bytes 557056 | tf_op jit(solution)/shard_map/reduce_scatter | solution.py:62
  226.6 43.2 %all-to-all-start.3 = ((bf16[16,2,128,128]{3,2,1,0:T(8,128)(2,1)}), bf16[16,2,128,128]{3,2,1,0:T(8,128)(2,1)S(1)}, u32[]{:S(2)}, u32[]{:S(2)}) async-start(bf16[16,2,128,128]{3,2,1,0:T(8,128)(2,1)} %slice.52), calls=%async_computation.3 | async-start | bytes 2097152 | tf_op jit(solution)/shard_map/all_to_all | solution.py:58
  241.4 60.3 %reduce-scatter.9.cloned.1.call-start = ((), (), s32[]{:S(2)}) async-start(), calls=%async_computation.7 | async-start | bytes 557056 | tf_op jit(solution)/shard_map/reduce_scatter | solution.py:62
Sparse Core Ops, SparseCore 0:
  102.0 56.7 reduce-scatter.6
  245.0 56.6 reduce-scatter.8

commit v8 on v6

--- a/solution.py
+++ b/solution.py
@@ -33,13 +33,14 @@
     dst_onehot = (
         jnp.arange(group_blocks, dtype=jnp.int32)[:, None] == tile_dst[0][None, :]
     ).astype(jnp.bfloat16)
+    usable = jnp.arange(capacity, dtype=jnp.int32)[None, :] < send_count[0][:, None]
+    pick_index = jnp.where(usable, jnp.clip(send_blocks[0], 0, own_blocks - 1), own_blocks)
     for layer in range(mix_weight.shape[0]):
         blocks = states.reshape(own_blocks, size_block, width) * active[layer][
             :, None, None
         ].astype(jnp.bfloat16)
-        usable = jnp.arange(capacity, dtype=jnp.int32)[None, :] < send_count[0][:, None]
-        picked = jnp.take(blocks, send_blocks[0], axis=0)
-        picked = jnp.where(usable[:, :, None, None], picked, jnp.zeros_like(picked))
+        with_zero = jnp.concatenate([blocks, jnp.zeros_like(blocks[:1])], axis=0)
+        picked = jnp.take(with_zero, pick_index, axis=0)
         arrived = lax.all_to_all(picked, "node", split_axis=0, concat_axis=0, tiled=True)
         slot_index = tile_node[0] * capacity + tile_block[0]
         source = arrived.reshape(-1, size_block, width)

time: 248 us -> 246 us (level)
  no operation moved by 1% of the time
where the time goes in v8:
time: 246 us
  waiting for transfers between devices  125 us (51%)
  blocking collectives  55.9 us (23%)
  starting transfers between devices  28.4 us (12%)
  matrix products  18.1 us (7%)
  local copies, waits for them, and re-layouts  12.4 us (5%)
  other arithmetic  5.99 us (2%)
    all_to_all x2, waiting for transfers between devices, body(): lax.all_to_all(partial_sum, 'tile', split_axis=0, concat_axis=0, tiled=True)  76.4 us
    all_to_all x1, blocking collectives, body(): lax.all_to_all(picked, 'node', split_axis=0, concat_axis=0, tiled=True)  55.9 us
    all_to_all x1, waiting for transfers between devices, body(): lax.all_to_all(picked, 'node', split_axis=0, concat_axis=0, tiled=True)  48.6 us
    all_to_all x2, starting transfers between devices, body(): lax.all_to_all(partial_sum, 'tile', split_axis=0, concat_axis=0, tiled=True)  17.9 us
    dot_general x2, matrix products, body(): jnp.einsum('tij,tjf->tfi', adjacency, modulated, preferred_element_type=j...  12 us
    all_to_all x1, starting transfers between devices, body(): lax.all_to_all(picked, 'node', split_axis=0, concat_axis=0, tiled=True)  10.5 us
    gather x2, local copies, waits for them, and re-layouts, body(): source_rows = jnp.take(source, slot_index, axis=0)  6.04 us
    dot_general x2, matrix products, body(): jnp.dot(dst_onehot, flat_products.astype(jnp.bfloat16), preferred_element...  5.44 us
  transfers between devices with their start and end apart: 3, of which 3 were waited for; matrix products, arithmetic and copies ran while one was open for 0% of the time, Pallas kernels for 0%

profile of v8, /device:TPU:1, one launch (start us, length us, event | category | flops | bytes accessed | tf_op | source)
XLA Modules:
  0.0 246.1 jit_solution(9117286049449899)
XLA Ops:
  0.0 0.7 convert.6
  0.7 0.7 compare_and_fusion.1
  1.7 1.0 broadcast_multiply_fusion.1
  2.7 1.0 gather_fusion
  3.7 1.6 broadcast_select_fusion.1
  5.3 10.5 %all-to-all-start = ((bf16[32,2,128,128]{3,2,1,0:T(8,128)(2,1)}), bf16[32,2,128,128]{3,2,1,0:T(8,128)(2,1)S(1)}, u32[]{:S(2)}, u32[]{:S(2)}) async-start(bf16[32,2,128,128]{3,2,1,0:T(8,128)(2,1)} %broadcast_select_fusion.1), calls=%async_computation | async-start | bytes 4194304 | tf_op jit(solution)/shard_map/all_to_all | solution.py:44
  16.1 48.6 %all-to-all-done = bf16[32,2,128,128]{3,2,1,0:T(8,128)(2,1)S(1)} async-done(((bf16[32,2,128,128]{3,2,1,0:T(8,128)(2,1)}), bf16[32,2,128,128]{3,2,1,0:T(8,128)(2,1)S(1)}, u32[]{:S(2)}, u32[]{:S(2)}) %all-to-all-start) | async-done | bytes 2097184 | tf_op jit(solution)/shard_map/all_to_all | solution.py:44
  64.7 3.0 %gather_fusion.1 = bf16[128,128,128]{2,1,0:T(8,128)(2,1)} fusion(bf16[64,128,128]{2,1,0:T(8,128)(2,1)S(1)} %bitcast.74, s32[1024]{0:T(1024)S(1)} %pad_clamp_fusion), kind=kCustom, calls=%fused_computation.1.clone | custom fusion | bytes 8389120 | tf_op jit(solution)/shard_map/jit(_take)/gather | solution.py:47
  67.7 6.0 %fusion.13 = bf16[128,128,128]{2,1,0:T(8,128)(2,1)S(1)} fusion(bf16[128,128,128]{2,1,0:T(8,128)(2,1)} %param.17, bf16[128,128,128]{2,1,0:T(8,128)(2,1)} %gather_fusion.1, f32[128,128]{1,0:T(8,128)S(1)} %fusion.22, pred[128]{0:T(512)(128)(4,1)S(1)} %get-tuple-element.6), kind=kOutput, calls=%fused_computation.21 | convolution fusion | flops 547356672 | bytes 12648576 | tf_op jit(solution)/shard_map/tij,tjf->tfi/dot_general | solution.py:49
  73.7 2.7 %fusion.16 = bf16[6,8,128,128]{3,1,2,0:T(8,128)(2,1)S(1)} fusion(bf16[16,8,128,128]{3,2,1,0:T(8,128)(2,1)S(1)} %bitcast.79, s32[128]{0:T(128)S(1)} %bitcast.90), kind=kOutput, calls=%fused_computation.26 | convolution fusion | flops 202119168 | bytes 5767680 | tf_op jit(solution)/shard_map/dot_general | solution.py:53
  76.5 1.6 copy.56
  78.1 12.4 %all-to-all-start.1 = ((bf16[16,3,128,128]{3,2,1,0:T(8,128)(2,1)}), bf16[16,3,128,128]{3,2,1,0:T(8,128)(2,1)S(1)}, u32[]{:S(2)}, u32[]{:S(2)}) async-start(bf16[16,3,128,128]{3,2,1,0:T(8,128)(2,1)} %bitcast.37), calls=%async_computation.1 | async-start | bytes 3145728 | tf_op jit(solution)/shard_map/all_to_all | solution.py:59
  91.0 38.0 %all-to-all-done.1 = bf16[16,3,128,128]{3,2,1,0:T(8,128)(2,1)S(1)} async-done(((bf16[16,3,128,128]{3,2,1,0:T(8,128)(2,1)}), bf16[16,3,128,128]{3,2,1,0:T(8,128)(2,1)S(1)}, u32[]{:S(2)}, u32[]{:S(2)}) %all-to-all-start.1) | async-done | bytes 1572896 | tf_op jit(solution)/shard_map/all_to_all | solution.py:59
  130.1 1.0 gather_fusion.2
  131.0 0.3 broadcast_select_fusion
  131.3 55.9 %all_to_all.20 = bf16[32,2,128,128]{3,2,1,0:T(8,128)(2,1)S(1)} all-to-all(bf16[32,2,128,128]{3,2,1,0:T(8,128)(2,1)S(1)} %broadcast_select_fusion), channel_id=1, replica_groups=mesh['node'=32,'tile'=16] {'node'}, dimensions={0} | all-to-all | bytes 4194304 | tf_op jit(solution)/shard_map/all_to_all | solution.py:44
  187.2 3.0 %gather_fusion.3 = bf16[128,128,128]{2,1,0:T(8,128)(2,1)} fusion(bf16[64,128,128]{2,1,0:T(8,128)(2,1)S(1)} %bitcast.75, s32[1024]{0:T(1024)S(1)} %pad_clamp_fusion), kind=kCustom, calls=%fused_computation.3.clone | custom fusion | bytes 8389120 | tf_op jit(solution)/shard_map/jit(_take)/gather | solution.py:47
  190.2 6.0 %fusion.12 = bf16[128,128,128]{2,1,0:T(8,128)(2,1)S(1)} fusion(bf16[128,128,128]{2,1,0:T(8,128)(2,1)} %param.17, bf16[128,128,128]{2,1,0:T(8,128)(2,1)} %gather_fusion.3, f32[128,128]{1,0:T(8,128)S(1)} %fusion.22, pred[128]{0:T(512)(128)(4,1)S(1)} %get-tuple-element.6), kind=kOutput, calls=%fused_computation.20 | convolution fusion | flops 547356672 | bytes 12648576 | tf_op jit(solution)/shard_map/tij,tjf->tfi/dot_general | solution.py:49
  196.2 2.7 %fusion.19 = bf16[6,8,128,128]{3,1,2,0:T(8,128)(2,1)S(1)} fusion(bf16[16,8,128,128]{3,2,1,0:T(8,128)(2,1)S(1)} %bitcast.78, s32[128]{0:T(128)S(1)} %bitcast.91), kind=kOutput, calls=%fused_computation.27 | convolution fusion | flops 202119168 | bytes 5767680 | tf_op jit(solution)/shard_map/dot_general | solution.py:53
  198.9 1.6 copy.58
  200.5 5.5 %all-to-all-start.3 = ((bf16[16,3,128,128]{3,2,1,0:T(8,128)(2,1)}), bf16[16,3,128,128]{3,2,1,0:T(8,128)(2,1)S(1)}, u32[]{:S(2)}, u32[]{:S(2)}) async-start(bf16[16,3,128,128]{3,2,1,0:T(8,128)(2,1)} %bitcast.43), calls=%async_computation.3 | async-start | bytes 3145728 | tf_op jit(solution)/shard_map/all_to_all | solution.py:59
  206.1 38.4 %all-to-all-done.3 = bf16[16,3,128,128]{3,2,1,0:T(8,128)(2,1)S(1)} async-done(((bf16[16,3,128,128]{3,2,1,0:T(8,128)(2,1)}), bf16[16,3,128,128]{3,2,1,0:T(8,128)(2,1)S(1)}, u32[]{:S(2)}, u32[]{:S(2)}) %all-to-all-start.3) | async-done | bytes 1572896 | tf_op jit(solution)/shard_map/all_to_all | solution.py:59
  244.5 0.3 reduce_sum.63
  245.4 0.7 add_convert_fusion
  (51 shorter events, 2.8 us)
Async XLA Ops:
  0.0 15.8 %copy-start = (bf16[535,128]{1,0:T(8,128)(2,1)S(1)}, bf16[535,128]{1,0:T(8,128)(2,1)}, u32[]{:S(2)}) copy-start(bf16[535,128]{1,0:T(8,128)(2,1)} %param.25) | copy-start | bytes 410884
  3.7 12.1 %copy-start.5 = (s32[1,128]{1,0:T(1,128)S(1)}, s32[1,128]{1,0:T(1,128)}, u32[]{:S(2)}) copy-start(s32[1,128]{1,0:T(1,128)} %param.19) | copy-start | bytes 1540
  3.7 12.1 %copy-start.6 = (s32[1,128]{1,0:T(1,128)S(1)}, s32[1,128]{1,0:T(1,128)}, u32[]{:S(2)}) copy-start(s32[1,128]{1,0:T(1,128)} %param.18) | copy-start | bytes 1540
  3.7 12.2 %copy-start.7 = (s32[1,128]{1,0:T(1,128)S(1)}, s32[1,128]{1,0:T(1,128)}, u32[]{:S(2)}) copy-start(s32[1,128]{1,0:T(1,128)} %param.20) | copy-start | bytes 1540
  5.3 59.4 %all-to-all-start = ((bf16[32,2,128,128]{3,2,1,0:T(8,128)(2,1)}), bf16[32,2,128,128]{3,2,1,0:T(8,128)(2,1)S(1)}, u32[]{:S(2)}, u32[]{:S(2)}) async-start(bf16[32,2,128,128]{3,2,1,0:T(8,128)(2,1)} %broadcast_select_fusion.1), calls=%async_computation | async-start | bytes 4194304 | tf_op jit(solution)/shard_map/all_to_all | solution.py:44
  67.7 6.0 %copy-start.3 = (s32[1,128]{1,0:T(1,128)S(1)}, s32[1,128]{1,0:T(1,128)}, u32[]{:S(2)}) copy-start(s32[1,128]{1,0:T(1,128)} %param.21) | copy-start | bytes 1540
  76.5 14.0 %copy-start.2 = (bf16[2,64,64]{2,1,0:T(8,128)(2,1)S(1)}, bf16[2,64,64]{2,1,0:T(8,128)(2,1)}, u32[]{:S(2)}) copy-start(bf16[2,64,64]{2,1,0:T(8,128)(2,1)} %param.26) | copy-start | bytes 49156
  76.5 14.5 %copy-start.4 = (f32[2,64]{1,0:T(2,128)S(1)}, f32[2,64]{1,0:T(2,128)}, u32[]{:S(2)}) copy-start(f32[2,64]{1,0:T(2,128)} %param.27) | copy-start | bytes 1540
  76.5 53.4 %copy-start.1 = (bf16[384,128]{1,0:T(8,128)(2,1)S(1)}, bf16[384,128]{1,0:T(8,128)(2,1)}, u32[]{:S(2)}) copy-start(bf16[384,128]{1,0:T(8,128)(2,1)} %param.16) | copy-start | bytes 294916
  78.1 51.0 %all-to-all-start.1 = ((bf16[16,3,128,128]{3,2,1,0:T(8,128)(2,1)}), bf16[16,3,128,128]{3,2,1,0:T(8,128)(2,1)S(1)}, u32[]{:S(2)}, u32[]{:S(2)}) async-start(bf16[16,3,128,128]{3,2,1,0:T(8,128)(2,1)} %bitcast.37), calls=%async_computation.1 | async-start | bytes 3145728 | tf_op jit(solution)/shard_map/all_to_all | solution.py:59
  200.5 44.0 %all-to-all-start.3 = ((bf16[16,3,128,128]{3,2,1,0:T(8,128)(2,1)}), bf16[16,3,128,128]{3,2,1,0:T(8,128)(2,1)S(1)}, u32[]{:S(2)}, u32[]{:S(2)}) async-start(bf16[16,3,128,128]{3,2,1,0:T(8,128)(2,1)} %bitcast.43), calls=%async_computation.3 | async-start | bytes 3145728 | tf_op jit(solution)/shard_map/all_to_all | solution.py:59
